TPU v7x, 768 devices: a whole 4x8x12 slice. The times are simulated.
768 devices in a mesh: dp: 96 (over z, y), tensor: 8 (over x, core).
Axes of the slice: x: 4, y: 8, z: 12, core: 2. Of those that a mesh axis runs over, the one named last changes fastest.
Arguments:
- tokens: bfloat16 [12288, 2048], P('dp', 'tensor'), may hold values from -6 to 6
- cotangent: bfloat16 [12288, 2048], P('dp', 'tensor'), may hold values from -6 to 6
- pair_ids: int32 [12288], P('dp'), may hold values from 0 to 99, as said below
- up_mask: int32 [100, 16, 64], P(None, None, 'tensor'), may hold values 0 or 1
- down_mask: int32 [100, 64, 16], P(None, 'tensor'), may hold values 0 or 1
- up_weight: bfloat16 [2048, 8192], P(None, 'tensor'), may hold values from -0.125 to 0.125
- down_weight: bfloat16 [96, 8192, 2048], P('dp', 'tensor'), may hold values from -0.0625 to 0.0625
Outputs:
- mixed: bfloat16 [12288, 2048], P('dp', 'tensor')
- token_grads: bfloat16 [12288, 2048], P('dp', 'tensor')
Inputs may be any that keep to these rules, and one draw needn't show every extreme that they name: `pair_ids`: within each aligned block of 128 tokens (the tokens of one index of dp) at most 2 tokens belong to one language group; in every draw 8 groups hold exactly 2 tokens of every block.
All inputs are finite; a program needn't handle non-finite values. No bound on the sum of `up_mask` or of `down_mask` on one device may be relied on, other than what follows from the above.
Results may differ from a plain program's by a relative error of at most 0.014.
Values may be sent and summed in bfloat16 or wider, within the bound.
No kernel may reach another device: no remote copies, remote signals or barrier semaphores. Data moves between devices by JAX's collectives and lax.ppermute only.
A program may use at most 128 MiB of HBM per device.

v0:
```python
import jax
import jax.numpy as jnp
from jax import lax
from jax.sharding import PartitionSpec as P

BLOCK = 128


def as_sent(x):

    def short(part):
        return part.astype(jnp.bfloat16) if part.dtype == jnp.float32 else part

    return jax.tree.map(short, x)


def row_masks(mask_table, pairs_here):
    pair_count = mask_table.shape[0]
    picker = (pairs_here[:, None] == jnp.arange(pair_count, dtype=jnp.int32)[None, :]).astype(
        jnp.bfloat16
    )
    flattened = mask_table.reshape(pair_count, -1).astype(jnp.bfloat16)
    looked = jnp.dot(picker, flattened, preferred_element_type=jnp.float32).astype(jnp.bfloat16)
    return looked.reshape(pairs_here.shape[0], mask_table.shape[1], mask_table.shape[2])


def masked_inputs(inputs, block_masks):
    row_count = inputs.shape[0]
    width = inputs.shape[1]
    blocks_in = block_masks.shape[2]
    blocks_out = block_masks.shape[0]
    pieces = inputs.reshape(row_count, blocks_in, width // blocks_in)
    masked = pieces[None, :, :, :] * block_masks[:, :, :, None]
    return masked.reshape(blocks_out, row_count, width)


def product_plain(inputs, weight, masks):
    columns = weight.shape[1]
    blocks_out = columns // BLOCK
    masked = masked_inputs(inputs, jnp.transpose(masks, (2, 0, 1)))
    weight_tiles = weight.reshape(weight.shape[0], blocks_out, BLOCK)
    result = jnp.einsum("nrk,knc->rnc", masked, weight_tiles, preferred_element_type=jnp.float32)
    return result.reshape(inputs.shape[0], columns)


def product_turned(inputs, weight, masks):
    columns = weight.shape[0]
    blocks_out = columns // BLOCK
    masked = masked_inputs(inputs, jnp.transpose(masks, (1, 0, 2)))
    weight_tiles = weight.reshape(blocks_out, BLOCK, weight.shape[1])
    result = jnp.einsum("nrk,nck->rnc", masked, weight_tiles, preferred_element_type=jnp.float32)
    return result.reshape(inputs.shape[0], columns)


def spread_rows(placer, values, groups, capacity):
    moved = jnp.dot(placer, values, preferred_element_type=jnp.float32).astype(jnp.bfloat16)
    return moved.reshape(groups, capacity, values.shape[1])


def route_grads(outgoing):
    return lax.all_to_all(outgoing, "dp", split_axis=0, concat_axis=0, tiled=True)


def widen(pieces):
    return jax.tree.map(
        lambda part, own: part.astype(own.dtype),
        lax.all_gather(as_sent(pieces), "tensor", axis=1, tiled=True),
        pieces,
    )


def settle(pieces):
    return jax.tree.map(
        lambda part: part.astype(jnp.float32),
        lax.psum_scatter(as_sent(pieces), "tensor", scatter_dimension=1, tiled=True),
    )


def send_back(values, placer, groups, capacity):
    returned = lax.all_to_all(
        values.reshape(groups, capacity, values.shape[1]),
        "dp",
        split_axis=0,
        concat_axis=0,
        tiled=True,
    )
    flattened = returned.reshape(groups * capacity, values.shape[1])
    return jnp.dot(placer.T, flattened, preferred_element_type=jnp.float32).astype(jnp.bfloat16)


def per_device(tokens, cotangent, pair_ids, up_mask, down_mask, up_weight, down_weight):
    groups = lax.axis_size("dp")
    tok_count = pair_ids.shape[0]
    capacity = max(2, (3 * tok_count + 2 * groups - 1) // (2 * groups))
    slot_count = groups * capacity
    target = pair_ids % groups
    matches = (target[:, None] == jnp.arange(groups, dtype=jnp.int32)[None, :]).astype(jnp.int32)
    before = jnp.sum((jnp.cumsum(matches, axis=0) - matches) * matches, axis=1)
    position = target * capacity + before
    placing = position[None, :] == jnp.arange(slot_count, dtype=jnp.int32)[:, None]
    placer = placing.astype(jnp.bfloat16)
    slot_pairs = jnp.sum(jnp.where(placing, pair_ids[None, :] + 1, 0), axis=1) - 1
    outgoing = spread_rows(placer, tokens, groups, capacity)
    arrived, arrived_pairs = (
        lax.all_to_all(outgoing, "dp", split_axis=0, concat_axis=0, tiled=True),
        lax.all_to_all(
            slot_pairs.reshape(groups, capacity), "dp", split_axis=0, concat_axis=0, tiled=True
        ),
    )
    pairs_here = arrived_pairs.reshape(-1)
    up_rows = row_masks(up_mask, pairs_here)
    down_rows = row_masks(down_mask, pairs_here)
    down_local = down_weight[0]
    grads_out = spread_rows(placer, cotangent, groups, capacity)
    (gathered,) = widen((arrived.reshape(slot_count, -1),))
    before_act = product_plain(gathered, up_weight, up_rows)
    activated, backward_function = jax.vjp(jax.nn.gelu, before_act)
    hidden = activated.astype(jnp.bfloat16)
    blended_portion, backward_function = (
        product_plain(hidden, down_local, down_rows).astype(jnp.bfloat16),
        backward_function,
    )
    (mixed_sum,) = settle((blended_portion,))
    arrived_grads = route_grads(grads_out)
    (grad_rows,) = widen((arrived_grads.reshape(slot_count, -1),))
    grad_hidden = product_turned(grad_rows, down_local, down_rows)
    grad_pre = backward_function(grad_hidden)[0].astype(jnp.bfloat16)
    input_part = product_turned(grad_pre, up_weight, up_rows).astype(jnp.bfloat16)
    (input_sum,) = settle((input_part,))
    mixed = send_back(mixed_sum.astype(jnp.bfloat16), placer, groups, capacity)
    token_grads = send_back(input_sum.astype(jnp.bfloat16), placer, groups, capacity)
    return (mixed, token_grads)


def solution(mesh):
    return jax.shard_map(
        per_device,
        mesh=mesh,
        in_specs=(
            P("dp", "tensor"),
            P("dp", "tensor"),
            P("dp"),
            P(None, None, "tensor"),
            P(None, "tensor", None),
            P(None, "tensor"),
            P("dp", "tensor", None),
        ),
        out_specs=(P("dp", "tensor"), P("dp", "tensor")),
        check_vma=False,
    )
```

profile of v0, /device:TPU:8, one launch (start us, length us, event | category | flops | bytes accessed | tf_op | source)
XLA Modules:
  0.0 280.9 jit_solution(14776836601869576629)
XLA Ops:
  9.2 21.8 %all-to-all-start.1 = ((s32[96,1,2]{2,1,0:T(1,128)}), s32[96,1,2]{2,1,0:T(1,128)S(1)}, u32[]{:S(2)}, u32[]{:S(2)}) async-start(s32[96,1,2]{2,1,0:T(1,128)} %bitcast), calls=%async_computation.1 | async-start | bytes 98304 | tf_op jit(solution)/shard_map/all_to_all | solution.py:106
  31.2 1.0 convolution_convert_fusion
  34.4 10.2 %all-to-all-done.1 = s32[96,1,2]{2,1,0:T(1,128)S(1)} async-done(((s32[96,1,2]{2,1,0:T(1,128)}), s32[96,1,2]{2,1,0:T(1,128)S(1)}, u32[]{:S(2)}, u32[]{:S(2)}) %all-to-all-start.1) | async-done | bytes 800 | tf_op jit(solution)/shard_map/all_to_all | solution.py:106
  44.6 6.3 %all-to-all-start = ((bf16[96,2,256]{2,1,0:T(2,128)(2,1)}), bf16[96,2,256]{2,1,0:T(2,128)(2,1)S(1)}, u32[]{:S(2)}, u32[]{:S(2)}) async-start(bf16[96,2,256]{2,1,0:T(2,128)(2,1)} %reshape.122), calls=%async_computation | async-start | bytes 196608 | tf_op jit(solution)/shard_map/all_to_all | solution.py:105
  52.4 1.0 convolution_convert_fusion.5
  53.8 5.4 %mul.154 = bf16[8,192,16,128]{3,2,1,0:T(8,128)(2,1)} broadcast(bf16[8,192,16]{2,1,0:T(8,128)(2,1)S(1)} %copy.42), dimensions={0,1,2} | broadcast | bytes 6340608 | tf_op jit(solution)/shard_map/mul | solution.py:33
  59.2 10.3 %mul.155 = bf16[8,192,2048]{2,1,0:T(8,128)(2,1)} reshape(bf16[8,192,16,128]{3,2,1,0:T(8,128)(2,1)} %mul.154) | data formatting | bytes 12582912 | tf_op jit(solution)/shard_map/mul | solution.py:33
  70.1 5.5 %mul.167 = bf16[8,192,16,128]{3,2,1,0:T(8,128)(2,1)} broadcast(bf16[8,192,16]{2,1,0:T(8,128)(2,1)S(1)} %copy.49), dimensions={0,1,2} | broadcast | bytes 6340608 | tf_op jit(solution)/shard_map/mul | solution.py:33
  75.5 10.3 %mul.168 = bf16[8,192,2048]{2,1,0:T(8,128)(2,1)} reshape(bf16[8,192,16,128]{3,2,1,0:T(8,128)(2,1)} %mul.167) | data formatting | bytes 12582912 | tf_op jit(solution)/shard_map/mul | solution.py:33
  86.2 5.4 %mul.183 = bf16[16,192,8,128]{3,2,1,0:T(8,128)(2,1)} broadcast(bf16[16,192,8]{2,1,0:T(8,128)(2,1)S(1)} %copy.51), dimensions={0,1,2} | broadcast | bytes 6340608 | tf_op jit(solution)/shard_map/mul | solution.py:33
  91.7 10.3 %mul.184 = bf16[16,192,1024]{2,1,0:T(8,128)(2,1)} reshape(bf16[16,192,8,128]{3,2,1,0:T(8,128)(2,1)} %mul.183) | data formatting | bytes 12582912 | tf_op jit(solution)/shard_map/mul | solution.py:33
  102.0 15.7 %all-to-all-start.3 = ((bf16[96,2,256]{2,1,0:T(2,128)(2,1)}), bf16[96,2,256]{2,1,0:T(2,128)(2,1)S(1)}, u32[]{:S(2)}, u32[]{:S(2)}) async-start(bf16[96,2,256]{2,1,0:T(2,128)(2,1)} %reshape.129), calls=%async_computation.4 | async-start | bytes 196608 | tf_op jit(solution)/shard_map/all_to_all | solution.py:61
  117.8 13.8 %all_gather.6 = bf16[192,2048]{1,0:T(8,128)(2,1)S(1)} all-gather(bf16[192,256]{1,0:T(8,128)(2,1)S(1)} %reshape.123), channel_id=1, replica_groups=mesh['dp'=96,'tensor'=8] {'tensor'}, dimensions={1}, use_global_device_ids=true | all-gather | bytes 884736 | tf_op jit(solution)/shard_map/all_gather | solution.py:67
  132.0 14.0 %all_gather.7 = bf16[192,2048]{1,0:T(8,128)(2,1)S(1)} all-gather(bf16[192,256]{1,0:T(8,128)(2,1)S(1)} %reshape.130), channel_id=1, replica_groups=mesh['dp'=96,'tensor'=8] {'tensor'}, dimensions={1}, use_global_device_ids=true | all-gather | bytes 884736 | tf_op jit(solution)/shard_map/all_gather | solution.py:67
  146.1 6.3 %fusion.28 = f32[192,8,128]{2,0,1:T(8,128)S(1)} fusion(bf16[8,192,2048]{2,1,0:T(8,128)(2,1)} %mul.155, bf16[192,2048]{1,0:T(8,128)(2,1)S(1)} %all_gather.6, bf16[2048,1024]{1,0:T(8,128)(2,1)} %param.12), kind=kOutput, calls=%fused_computation.18 | convolution fusion | flops 808452096 | bytes 12058624 | tf_op jit(solution)/shard_map/nrk,knc->rnc/dot_general | solution.py:42
  152.4 2.2 fusion.48
  154.7 4.1 %fusion.33 = bf16[16,24,8,128]{3,2,1,0:T(8,128)(2,1)S(1)} fusion(bf16[16,128,1024]{2,1,0:T(8,128)(2,1)} %bitcast.89, bf16[16,192,1024]{2,1,0:T(8,128)(2,1)S(1)} %bitcast.77, bf16[192,1024]{1,0:T(8,128)(2,1)S(1)} %bitcast.87), kind=kOutput, calls=%fused_computation.19 | convolution fusion | flops 808845312 | bytes 11665408 | tf_op jit(solution)/shard_map/nrk,nck->rnc/dot_general | solution.py:51
  158.8 1.1 copy.75
  160.2 5.5 %copy.58 = bf16[128,8,16,128]{3,2,1,0:T(8,128)(2,1)} copy(bf16[128,8,16,128]{3,1,2,0:T(8,128)(2,1)} %bitcast.78) | data formatting | bytes 8388608
  166.1 5.5 %mul.163 = bf16[16,192,8,128]{3,2,1,0:T(8,128)(2,1)} broadcast(bf16[16,192,8]{2,1,0:T(8,128)(2,1)S(1)} %copy.46), dimensions={0,1,2} | broadcast | bytes 6340608 | tf_op jit(solution)/shard_map/mul | solution.py:33
  171.6 10.3 %mul.164 = bf16[16,192,1024]{2,1,0:T(8,128)(2,1)} reshape(bf16[16,192,8,128]{3,2,1,0:T(8,128)(2,1)} %mul.163) | data formatting | bytes 12582912 | tf_op jit(solution)/shard_map/mul | solution.py:33
  182.2 7.3 %fusion.23 = bf16[16,24,8,128]{3,2,1,0:T(8,128)(2,1)S(1)} fusion(bf16[1024,16,128]{2,1,0:T(8,128)(2,1)} %bitcast.80, bf16[16,192,1024]{2,1,0:T(8,128)(2,1)} %mul.164, bf16[192,1024]{1,0:T(8,128)(2,1)S(1)} %copy_bitcast_fusion.3), kind=kOutput, calls=%fused_computation.17 | convolution fusion | flops 808845312 | bytes 11665408 | tf_op jit(solution)/shard_map/nrk,knc->rnc/dot_general | solution.py:42
  189.5 1.1 copy.76
  190.7 8.3 %reduce-scatter.5.cloned.1.call-done = bf16[192,256]{1,0:T(8,128)(2,1)} async-done(((bf16[192,2048]{1,0:T(8,128)(2,1)}), bf16[192,256]{1,0:T(8,128)(2,1)}) %reduce-scatter.5.cloned.1.call-update) | async-done | bytes 98320 | tf_op jit(solution)/shard_map/reduce_scatter | solution.py:75
  198.9 1.6 reshape.132
  200.5 16.5 %all-to-all-start.4 = ((bf16[96,2,256]{2,1,0:T(2,128)(2,1)}), bf16[96,2,256]{2,1,0:T(2,128)(2,1)S(1)}, u32[]{:S(2)}, u32[]{:S(2)}) async-start(bf16[96,2,256]{2,1,0:T(2,128)(2,1)} %reshape.132), calls=%async_computation.6 | async-start | bytes 196608 | tf_op jit(solution)/shard_map/all_to_all | solution.py:80
  217.0 24.1 %reduce-scatter.3.cloned.1.call-done = bf16[192,256]{1,0:T(8,128)(2,1)} async-done(((bf16[192,2048]{1,0:T(8,128)(2,1)}), bf16[192,256]{1,0:T(8,128)(2,1)}) %reduce-scatter.3.cloned.1.call-update) | async-done | bytes 98320 | tf_op jit(solution)/shard_map/reduce_scatter | solution.py:75
  241.1 1.6 reshape.127
  242.7 16.2 %all-to-all-start.2 = ((bf16[96,2,256]{2,1,0:T(2,128)(2,1)}), bf16[96,2,256]{2,1,0:T(2,128)(2,1)S(1)}, u32[]{:S(2)}, u32[]{:S(2)}) async-start(bf16[96,2,256]{2,1,0:T(2,128)(2,1)} %reshape.127), calls=%async_computation.3 | async-start | bytes 196608 | tf_op jit(solution)/shard_map/all_to_all | solution.py:80
  258.9 0.9 convolution_convert_fusion.2
  259.8 13.3 %all-to-all-done.2 = bf16[96,2,256]{2,1,0:T(2,128)(2,1)S(1)} async-done(((bf16[96,2,256]{2,1,0:T(2,128)(2,1)}), bf16[96,2,256]{2,1,0:T(2,128)(2,1)S(1)}, u32[]{:S(2)}, u32[]{:S(2)}) %all-to-all-start.2) | async-done | bytes 98336 | tf_op jit(solution)/shard_map/all_to_all | solution.py:80
  273.2 0.9 convolution_convert_fusion.3
  (51 shorter events, 8.7 us)
Async XLA Ops:
  7.2 23.8 %copy-start = (bf16[128,256]{1,0:T(8,128)(2,1)S(1)}, bf16[128,256]{1,0:T(8,128)(2,1)}, u32[]{:S(2)}) copy-start(bf16[128,256]{1,0:T(8,128)(2,1)} %param.7) | copy-start | bytes 196612
  9.2 35.4 %all-to-all-start.1 = ((s32[96,1,2]{2,1,0:T(1,128)}), s32[96,1,2]{2,1,0:T(1,128)S(1)}, u32[]{:S(2)}, u32[]{:S(2)}) async-start(s32[96,1,2]{2,1,0:T(1,128)} %bitcast), calls=%async_computation.1 | async-start | bytes 98304 | tf_op jit(solution)/shard_map/all_to_all | solution.py:106
  44.6 57.4 %all-to-all-start = ((bf16[96,2,256]{2,1,0:T(2,128)(2,1)}), bf16[96,2,256]{2,1,0:T(2,128)(2,1)S(1)}, u32[]{:S(2)}, u32[]{:S(2)}) async-start(bf16[96,2,256]{2,1,0:T(2,128)(2,1)} %reshape.122), calls=%async_computation | async-start | bytes 196608 | tf_op jit(solution)/shard_map/all_to_all | solution.py:105
  102.0 30.0 %all-to-all-start.3 = ((bf16[96,2,256]{2,1,0:T(2,128)(2,1)}), bf16[96,2,256]{2,1,0:T(2,128)(2,1)S(1)}, u32[]{:S(2)}, u32[]{:S(2)}) async-start(bf16[96,2,256]{2,1,0:T(2,128)(2,1)} %reshape.129), calls=%async_computation.4 | async-start | bytes 196608 | tf_op jit(solution)/shard_map/all_to_all | solution.py:61
  117.7 81.2 %reduce-scatter.5.cloned.1.call-start = ((), (), s32[]{:S(2)}) async-start(), calls=%async_computation.8 | async-start | bytes 884736 | tf_op jit(solution)/shard_map/reduce_scatter | solution.py:75
  132.0 20.4 %slice-start = ((s8[6291456]{0:T(1024)(128)(4,1)}), s8[4194304]{0:T(1024)(128)(4,1)S(1)}, s32[]{:S(2)}) async-start(s8[6291456]{0:T(1024)(128)(4,1)} %bitcast.74), calls=%async_computation.9 | async-start | bytes 8388608
  146.1 6.3 %slice-start.1 = ((s8[6291456]{0:T(1024)(128)(4,1)}), s8[2097152]{0:T(1024)(128)(4,1)S(1)}, s32[]{:S(2)}) async-start(s8[6291456]{0:T(1024)(128)(4,1)} %bitcast.74), calls=%async_computation.10 | async-start | bytes 4194304
  146.1 6.3 %copy-start.2 = (bf16[1,1024,2048]{2,1,0:T(8,128)(2,1)S(1)}, bf16[1,1024,2048]{2,1,0:T(8,128)(2,1)}, u32[]{:S(2)}) copy-start(bf16[1,1024,2048]{2,1,0:T(8,128)(2,1)} %param.13) | copy-start | bytes 12582916
  146.1 8.6 %slice-start.2 = ((s8[6291456]{0:T(1024)(128)(4,1)}), s8[4194304]{0:T(1024)(128)(4,1)S(1)}, s32[]{:S(2)}) async-start(s8[6291456]{0:T(1024)(128)(4,1)} %bitcast.76), calls=%async_computation.11 | async-start | bytes 8388608
  152.4 2.3 slice-start.3
  159.9 81.2 %reduce-scatter.3.cloned.1.call-start = ((), (), s32[]{:S(2)}) async-start(), calls=%async_computation.7 | async-start | bytes 884736 | tf_op jit(solution)/shard_map/reduce_scatter | solution.py:75
  182.2 91.8 %copy-start.1 = (bf16[128,256]{1,0:T(8,128)(2,1)S(1)}, bf16[128,256]{1,0:T(8,128)(2,1)}, u32[]{:S(2)}) copy-start(bf16[128,256]{1,0:T(8,128)(2,1)} %param.7) | copy-start | bytes 196612
  200.5 42.2 %all-to-all-start.4 = ((bf16[96,2,256]{2,1,0:T(2,128)(2,1)}), bf16[96,2,256]{2,1,0:T(2,128)(2,1)S(1)}, u32[]{:S(2)}, u32[]{:S(2)}) async-start(bf16[96,2,256]{2,1,0:T(2,128)(2,1)} %reshape.132), calls=%async_computation.6 | async-start | bytes 196608 | tf_op jit(solution)/shard_map/all_to_all | solution.py:80
  242.7 30.4 %all-to-all-start.2 = ((bf16[96,2,256]{2,1,0:T(2,128)(2,1)}), bf16[96,2,256]{2,1,0:T(2,128)(2,1)S(1)}, u32[]{:S(2)}, u32[]{:S(2)}) async-start(bf16[96,2,256]{2,1,0:T(2,128)(2,1)} %reshape.127), calls=%async_computation.3 | async-start | bytes 196608 | tf_op jit(solution)/shard_map/all_to_all | solution.py:80
Sparse Core Ops, SparseCore 0:
  160.0 38.8 reduce-scatter.4
  202.0 39.0 reduce-scatter.2
where the time goes:
time: 282 us; the launch traced here: 281 us
  local copies, waits for them, and re-layouts  78.5 us (28%)
  starting transfers between devices  76.8 us (27%)
  waiting for transfers between devices  56.4 us (20%)
  blocking collectives  27.8 us (10%)
  matrix products  24 us (9%)
  between operations  14.3 us (5%)
  other arithmetic  3.12 us (1%)
    mul x9, local copies, waits for them, and re-layouts, masked_inputs(): masked = pieces[None, :, :, :] * block_masks[:, :, :, None]  63.2 us
    all_to_all x2, starting transfers between devices, send_back(): lax.all_to_all(values.reshape(groups, capacity, values.shape[1]), 'dp', s...  32.7 us
    reduce_scatter x2, waiting for transfers between devices, settle(): lax.psum_scatter(as_sent(pieces), 'tensor', scatter_dimension=1, tiled=True)  32.4 us
    all_gather x2, blocking collectives, widen(): lax.all_gather(as_sent(pieces), 'tensor', axis=1, tiled=True)  27.8 us
    all_to_all x1, starting transfers between devices, per_device(): lax.all_to_all(slot_pairs.reshape(groups, capacity), 'dp', split_axis=0,...  21.8 us
    all_to_all x1, starting transfers between devices, route_grads(): lax.all_to_all(outgoing, 'dp', split_axis=0, concat_axis=0, tiled=True)  15.7 us
    dot_general x2, matrix products, product_plain(): jnp.einsum('nrk,knc->rnc', masked, weight_tiles, preferred_element_type=j...  13.6 us
    all_to_all x2, waiting for transfers between devices, send_back(): lax.all_to_all(values.reshape(groups, capacity, values.shape[1]), 'dp', s...  13.3 us
  transfers between devices with their start and end apart: 7, of which 5 were waited for; matrix products, arithmetic and copies ran while one was open for 32% of the time, Pallas kernels for 0%

commit v1 on v0

v1 whole, which is shorter than its diff:
```python
import functools

import jax
import jax.numpy as jnp
from jax import lax
from jax.experimental import pallas as pl
from jax.sharding import PartitionSpec as P

BLOCK = 128
STEPS = 4


def picked_masks(mask_table, pairs_here, order):
    table = jnp.transpose(mask_table, order)
    pair_count, blocks_out, blocks_in = table.shape
    table = jnp.pad(table, ((0, 0), (0, 0), (0, BLOCK - blocks_in)))
    picker = (pairs_here[:, None] == jnp.arange(pair_count, dtype=jnp.int32)[None, :]).astype(
        jnp.bfloat16
    )
    flattened = table.reshape(pair_count, -1).astype(jnp.bfloat16)
    looked = jnp.dot(picker, flattened, preferred_element_type=jnp.float32).astype(jnp.bfloat16)
    looked = looked.reshape(pairs_here.shape[0], blocks_out, BLOCK)
    return jnp.transpose(looked, (1, 0, 2)), blocks_in


def masked_kernel(x_ref, m_ref, e_ref, w_ref, o_ref, *, per, turned):
    x = x_ref[...]
    for b in range(per):
        spread = jnp.dot(m_ref[b], e_ref[...], preferred_element_type=jnp.float32)
        masked = x * spread.astype(x.dtype)
        if turned:
            w = w_ref[b * BLOCK:(b + 1) * BLOCK, :]
            acc = lax.dot_general(
                masked, w, (((1,), (1,)), ((), ())), preferred_element_type=jnp.float32
            )
        else:
            w = w_ref[:, b * BLOCK:(b + 1) * BLOCK]
            acc = jnp.dot(masked, w, preferred_element_type=jnp.float32)
        o_ref[:, b * BLOCK:(b + 1) * BLOCK] = acc.astype(o_ref.dtype)


def masked_product(x, masks, blocks_in, weight, turned, out_dtype):
    rows, width = x.shape
    blocks_out = masks.shape[0]
    per = max(1, blocks_out // STEPS)
    steps = blocks_out // per
    cols = per * BLOCK
    blk = width // blocks_in
    expand = (
        jnp.arange(width, dtype=jnp.int32)[None, :] // blk == jnp.arange(BLOCK, dtype=jnp.int32)[:, None]
    ).astype(x.dtype)
    if turned:
        w_spec = pl.BlockSpec((cols, width), lambda j: (j, 0))
    else:
        w_spec = pl.BlockSpec((width, cols), lambda j: (0, j))
    return pl.pallas_call(
        functools.partial(masked_kernel, per=per, turned=turned),
        grid=(steps,),
        in_specs=[
            pl.BlockSpec((rows, width), lambda j: (0, 0)),
            pl.BlockSpec((per, rows, BLOCK), lambda j: (j, 0, 0)),
            pl.BlockSpec((BLOCK, width), lambda j: (0, 0)),
            w_spec,
        ],
        out_specs=pl.BlockSpec((rows, cols), lambda j: (0, j)),
        out_shape=jax.ShapeDtypeStruct((rows, blocks_out * BLOCK), out_dtype),
    )(x, masks, expand, weight)


def per_device(tokens, cotangent, pair_ids, up_mask, down_mask, up_weight, down_weight):
    groups = lax.axis_size("dp")
    tok_count, piece = tokens.shape
    capacity = max(2, (3 * tok_count + 2 * groups - 1) // (2 * groups))
    slot_count = groups * capacity
    target = pair_ids % groups
    matches = (target[:, None] == jnp.arange(groups, dtype=jnp.int32)[None, :]).astype(jnp.int32)
    before = jnp.sum((jnp.cumsum(matches, axis=0) - matches) * matches, axis=1)
    position = target * capacity + before
    placing = position[None, :] == jnp.arange(slot_count, dtype=jnp.int32)[:, None]
    placer = placing.astype(jnp.bfloat16)
    slot_pairs = jnp.sum(jnp.where(placing, pair_ids[None, :] + 1, 0), axis=1) - 1

    payload = jnp.concatenate([tokens, cotangent], axis=1)
    outgoing = jnp.dot(placer, payload, preferred_element_type=jnp.float32).astype(jnp.bfloat16)
    pair_cols = jnp.broadcast_to(slot_pairs.astype(jnp.bfloat16)[:, None], (slot_count, BLOCK))
    outgoing = jnp.concatenate([outgoing, pair_cols], axis=1)
    arrived = lax.all_to_all(
        outgoing.reshape(groups, capacity, -1), "dp", split_axis=0, concat_axis=0, tiled=True
    ).reshape(slot_count, -1)
    pairs_here = arrived[:, 2 * piece].astype(jnp.int32)

    both = jnp.stack([arrived[:, :piece], arrived[:, piece:2 * piece]])
    gathered = lax.all_gather(both, "tensor", axis=2, tiled=True)
    rows_in, grad_rows = gathered[0], gathered[1]

    up_fwd, up_in = picked_masks(up_mask, pairs_here, (0, 2, 1))
    up_bwd, up_out = picked_masks(up_mask, pairs_here, (0, 1, 2))
    down_fwd, down_in = picked_masks(down_mask, pairs_here, (0, 2, 1))
    down_bwd, down_out = picked_masks(down_mask, pairs_here, (0, 1, 2))
    down_local = down_weight[0]

    before_act = masked_product(rows_in, up_fwd, up_in, up_weight, False, jnp.float32)
    activated, backward_function = jax.vjp(jax.nn.gelu, before_act)
    hidden = activated.astype(jnp.bfloat16)
    mixed_part = masked_product(hidden, down_fwd, down_in, down_local, False, jnp.bfloat16)
    grad_hidden = masked_product(grad_rows, down_bwd, down_out, down_local, True, jnp.float32)
    grad_pre = backward_function(grad_hidden)[0].astype(jnp.bfloat16)
    input_part = masked_product(grad_pre, up_bwd, up_out, up_weight, True, jnp.bfloat16)

    parts = jnp.stack([mixed_part, input_part])
    summed = lax.psum_scatter(parts, "tensor", scatter_dimension=2, tiled=True)
    summed = summed.astype(jnp.float32).astype(jnp.bfloat16)

    back = jnp.transpose(summed, (1, 0, 2)).reshape(groups, capacity, 2 * piece)
    returned = lax.all_to_all(back, "dp", split_axis=0, concat_axis=0, tiled=True)
    flattened = returned.reshape(slot_count, 2 * piece)
    results = jnp.dot(placer.T, flattened, preferred_element_type=jnp.float32).astype(jnp.bfloat16)
    return (results[:, :piece], results[:, piece:])


def solution(mesh):
    return jax.shard_map(
        per_device,
        mesh=mesh,
        in_specs=(
            P("dp", "tensor"),
            P("dp", "tensor"),
            P("dp"),
            P(None, None, "tensor"),
            P(None, "tensor", None),
            P(None, "tensor"),
            P("dp", "tensor", None),
        ),
        out_specs=(P("dp", "tensor"), P("dp", "tensor")),
        check_vma=False,
    )
```

time: 282 us -> 195 us (0.69)
  the two profiles are of different devices: /device:TPU:8 before, /device:TPU:7 now
where the time goes in v1:
time: 195 us; the launch traced here: 194 us
  blocking collectives  71.1 us (36%)
  waiting for transfers between devices  59 us (30%)
  Pallas kernels  28 us (14%)
  between operations  14.3 us (7%)
  local copies, waits for them, and re-layouts  9.96 us (5%)
  other arithmetic  8.85 us (5%)
  matrix products  2.72 us (1%)
    reduce_scatter x1, waiting for transfers between devices, per_device(): summed = lax.psum_scatter(parts, 'tensor', scatter_dimension=2, tiled=True)  42.5 us
    all_to_all x1, blocking collectives, per_device(): lax.all_to_all(outgoing.reshape(groups, capacity, -1), 'dp', split_axis=0...  38.9 us
    all_to_all x1, blocking collectives, per_device(): lax.all_to_all(back, 'dp', split_axis=0, concat_axis=0, tiled=True)  32.3 us
    pallas_call x4, Pallas kernels, masked_product(): pl.pallas_call(functools.partial(masked_kernel, per=per, turned=turned),...  28 us
    all_gather x1, waiting for transfers between devices, per_device(): gathered = lax.all_gather(both, 'tensor', axis=2, tiled=True)  16.4 us
  transfers between devices with their start and end apart: 2, of which 2 were waited for; matrix products, arithmetic and copies ran while one was open for 4% of the time, Pallas kernels for 0%

profile of v1, /device:TPU:7, one launch (start us, length us, event | category | flops | bytes accessed | tf_op | source)
XLA Modules:
  0.0 194.0 jit_solution(630960833775219340)
XLA Ops:
  7.2 0.7 and_select_fusion
  8.0 0.2 reduce_window_sum.11
  8.1 0.2 select_reduce_fusion.1
  8.5 1.1 convolution_convert_fusion.4
  9.8 38.9 %all_to_all.10 = bf16[96,2,640]{2,1,0:T(2,128)(2,1)S(1)} all-to-all(bf16[96,2,640]{2,1,0:T(2,128)(2,1)S(1)} %reshape.118), channel_id=1, replica_groups=mesh['dp'=96,'tensor'=8] {'dp'}, dimensions={0} | all-to-all | bytes 491520 | tf_op jit(solution)/shard_map/all_to_all | solution.py:87
  48.8 0.7 pad_maximum_fusion.2
  49.6 0.2 copy.23
  50.0 0.4 copy.24
  50.8 0.8 fusion.12.e_ref
  51.6 0.9 fusion.4.e_ref
  52.6 0.3 fusion.3
  52.9 0.8 copy.37
  53.7 0.3 fusion.2
  54.1 0.8 copy.38
  54.9 0.4 fusion
  55.3 1.1 copy.36
  56.4 0.4 fusion.1
  56.8 1.1 copy.35
  57.9 16.4 %all-gather.2.cloned.1.call-done = bf16[2,192,2048]{2,1,0:T(8,128)(2,1)} async-done(((bf16[2,192,256]{2,1,0:T(8,128)(2,1)}), bf16[2,192,2048]{2,1,0:T(8,128)(2,1)}) %all-gather.2.cloned.1.call-update) | async-done | bytes 1572880 | tf_op jit(solution)/shard_map/all_gather | solution.py:93
  74.4 2.7 %slice_bitcast_fusion = (bf16[192,2048]{1,0:T(8,128)(2,1)}, bf16[192,2048]{1,0:T(8,128)(2,1)}) fusion(bf16[2,192,2048]{2,1,0:T(8,128)(2,1)} %all-gather.2.cloned.1.call-done), kind=kLoop, calls=%fused_computation.24 | loop fusion | bytes 3145728 | tf_op jit(solution)/shard_map/squeeze | solution.py:94
  77.1 7.0 %shard_map.88 = f32[192,1024]{1,0:T(8,128)} custom-call(bf16[192,2048]{1,0:T(8,128)(2,1)} %get-tuple-element.2.x_ref, bf16[8,192,128]{2,1,0:T(8,128)(2,1)} %bitcast.71, bf16[128,2048]{1,0:T(8,128)(2,1)} %fusion.4.e_ref, bf16[1024,2048]{1,0:T(8,128)(2,1)} %bitcast.61), custom_call_target="tpu_custom_call" | custom-call | tf_op jit(solution)/shard_map/pallas_call | solution.py:56
  84.1 6.9 %shard_map.86 = f32[192,1024]{1,0:T(8,128)} custom-call(bf16[192,2048]{1,0:T(8,128)(2,1)} %get-tuple-element.3.x_ref, bf16[8,192,128]{2,1,0:T(8,128)(2,1)} %bitcast.70, bf16[128,2048]{1,0:T(8,128)(2,1)} %fusion.4.e_ref, bf16[2048,1024]{1,0:T(8,128)(2,1)} %w_ref.3), custom_call_target="tpu_custom_call" | custom-call | tf_op jit(solution)/shard_map/pallas_call | solution.py:56
  91.0 2.6 %multiply_convert_fusion = (bf16[192,1024]{1,0:T(8,128)(2,1)}, bf16[192,1024]{1,0:T(8,128)(2,1)}) fusion(f32[192,1024]{1,0:T(8,128)} %shard_map.86, f32[192,1024]{1,0:T(8,128)S(1)} %copy-done), kind=kLoop, calls=%fused_computation.26 | loop fusion | flops 4325376 | bytes 2359296 | tf_op jit(solution)/shard_map/convert_element_type | solution.py:104
  93.6 7.1 %shard_map.87 = bf16[192,2048]{1,0:T(8,128)(2,1)} custom-call(bf16[192,1024]{1,0:T(8,128)(2,1)} %get-tuple-element.4.x_ref, bf16[16,192,128]{2,1,0:T(8,128)(2,1)} %bitcast.63, bf16[128,1024]{1,0:T(8,128)(2,1)} %fusion.12.e_ref, bf16[1024,2048]{1,0:T(8,128)(2,1)} %bitcast.62), custom_call_target="tpu_custom_call" | custom-call | tf_op jit(solution)/shard_map/pallas_call | solution.py:56
  100.7 7.0 %shard_map.89 = bf16[192,2048]{1,0:T(8,128)(2,1)} custom-call(bf16[192,1024]{1,0:T(8,128)(2,1)} %get-tuple-element.5.x_ref, bf16[16,192,128]{2,1,0:T(8,128)(2,1)} %bitcast.64, bf16[128,1024]{1,0:T(8,128)(2,1)} %fusion.12.e_ref, bf16[2048,1024]{1,0:T(8,128)(2,1)} %w_ref.3), custom_call_target="tpu_custom_call" | custom-call | tf_op jit(solution)/shard_map/pallas_call | solution.py:56
  107.7 2.4 %pad_maximum_fusion = bf16[2,192,2048]{2,1,0:T(8,128)(2,1)} fusion(bf16[1,192,2048]{2,1,0:T(8,128)(2,1)} %bitcast.66, bf16[1,192,2048]{2,1,0:T(8,128)(2,1)S(1)} %bitcast.65), kind=kLoop, calls=%fused_computation.2 | loop fusion | flops 786432 | bytes 3145728 | tf_op jit(solution)/shard_map/stack | solution.py:110
  110.1 42.5 %reduce-scatter.2.cloned.1.call-done = bf16[2,192,256]{2,1,0:T(8,128)(2,1)} async-done(((bf16[2,192,2048]{2,1,0:T(8,128)(2,1)}), bf16[2,192,256]{2,1,0:T(8,128)(2,1)}) %reduce-scatter.2.cloned.1.call-update) | async-done | bytes 196624 | tf_op jit(solution)/shard_map/reduce_scatter | solution.py:111
  152.7 1.1 copy.22
  153.8 0.1 reshape.124
  153.9 32.3 %all_to_all.11 = bf16[96,2,512]{2,1,0:T(2,128)(2,1)S(1)} all-to-all(bf16[96,2,512]{2,1,0:T(2,128)(2,1)S(1)} %reshape.124), channel_id=1, replica_groups=mesh['dp'=96,'tensor'=8] {'dp'}, dimensions={0} | all-to-all | bytes 393216 | tf_op jit(solution)/shard_map/all_to_all | solution.py:115
  186.3 0.2 convolution_convert_fusion.5
  186.5 0.7 fusion.30
  (37 shorter events, 1.4 us)
Async XLA Ops:
  7.2 67.2 %all-gather.2.cloned.1.call-start = ((), (), s32[]{:S(2)}) async-start(), calls=%async_computation.3 | async-start | bytes 1769472 | tf_op jit(solution)/shard_map/all_gather | solution.py:93
  9.5 40.0 %copy-start.3 = (s32[100,8,16]{0,2,1:T(8,128)S(1)}, s32[100,8,16]{0,2,1:T(8,128)}, u32[]{:S(2)}) copy-start(s32[100,8,16]{0,2,1:T(8,128)} %param.11) | copy-start | bytes 153604
  9.5 40.0 %copy-start.2 = (s32[100,16,8]{0,2,1:T(8,128)S(1)}, s32[100,16,8]{0,2,1:T(8,128)}, u32[]{:S(2)}) copy-start(s32[100,16,8]{0,2,1:T(8,128)} %param.10) | copy-start | bytes 153604
  49.5 103.2 %reduce-scatter.2.cloned.1.call-start = ((), (), s32[]{:S(2)}) async-start(), calls=%async_computation.4 | async-start | bytes 1769472 | tf_op jit(solution)/shard_map/reduce_scatter | solution.py:111
  84.1 6.9 %copy-start = (f32[192,1024]{1,0:T(8,128)S(1)}, f32[192,1024]{1,0:T(8,128)}, u32[]{:S(2)}) copy-start(f32[192,1024]{1,0:T(8,128)} %shard_map.88) | copy-start | bytes 2359300
  100.7 7.0 %copy-start.1 = (bf16[192,2048]{1,0:T(8,128)(2,1)S(1)}, bf16[192,2048]{1,0:T(8,128)(2,1)}, u32[]{:S(2)}) copy-start(bf16[192,2048]{1,0:T(8,128)(2,1)} %shard_map.87) | copy-start | bytes 2359300
Sparse Core Ops, SparseCore 0:
  49.6 24.6 all-gather.1
  110.2 42.3 reduce-scatter.1

commit v2 on v1

--- a/solution.py
+++ b/solution.py
@@ -26,8 +26,8 @@
 def masked_kernel(x_ref, m_ref, e_ref, w_ref, o_ref, *, per, turned):
     x = x_ref[...]
     for b in range(per):
-        spread = jnp.dot(m_ref[b], e_ref[...], preferred_element_type=jnp.float32)
-        masked = x * spread.astype(x.dtype)
+        spread = jnp.dot(m_ref[b], e_ref[...], preferred_element_type=jnp.float32).astype(x.dtype)
+        masked = x * spread
         if turned:
             w = w_ref[b * BLOCK:(b + 1) * BLOCK, :]
             acc = lax.dot_general(
@@ -82,15 +82,22 @@
 
     payload = jnp.concatenate([tokens, cotangent], axis=1)
     outgoing = jnp.dot(placer, payload, preferred_element_type=jnp.float32).astype(jnp.bfloat16)
-    pair_cols = jnp.broadcast_to(slot_pairs.astype(jnp.bfloat16)[:, None], (slot_count, BLOCK))
-    outgoing = jnp.concatenate([outgoing, pair_cols], axis=1)
-    arrived = lax.all_to_all(
-        outgoing.reshape(groups, capacity, -1), "dp", split_axis=0, concat_axis=0, tiled=True
-    ).reshape(slot_count, -1)
-    pairs_here = arrived[:, 2 * piece].astype(jnp.int32)
+    feat_rows = outgoing.reshape(groups, capacity * 2 * piece // BLOCK, BLOCK)
+    pair_rows = jnp.broadcast_to(
+        slot_pairs.astype(jnp.bfloat16).reshape(groups, capacity, 1), (groups, capacity, BLOCK)
+    )
+    used = feat_rows.shape[1] + capacity
+    tile_rows = -(-used // 16) * 16
+    filler = jnp.zeros((groups, tile_rows - used, BLOCK), jnp.bfloat16)
+    outgoing = jnp.concatenate([feat_rows, pair_rows, filler], axis=1)
+    arrived = lax.all_to_all(outgoing, "dp", split_axis=0, concat_axis=0, tiled=True)
+    feats = arrived[:, :feat_rows.shape[1], :].reshape(slot_count, 2 * piece)
+    pairs_here = arrived[:, feat_rows.shape[1]:used, 0].reshape(slot_count).astype(jnp.int32)
 
-    both = jnp.stack([arrived[:, :piece], arrived[:, piece:2 * piece]])
-    gathered = lax.all_gather(both, "tensor", axis=2, tiled=True)
+    both = jnp.stack([feats[:, :piece], feats[:, piece:]])
+    gathered = lax.all_gather(both, "tensor", axis=0, tiled=False)
+    shards = gathered.shape[0]
+    gathered = jnp.transpose(gathered, (1, 2, 0, 3)).reshape(2, slot_count, shards * piece)
     rows_in, grad_rows = gathered[0], gathered[1]
 
     up_fwd, up_in = picked_masks(up_mask, pairs_here, (0, 2, 1))
@@ -107,11 +114,12 @@
     grad_pre = backward_function(grad_hidden)[0].astype(jnp.bfloat16)
     input_part = masked_product(grad_pre, up_bwd, up_out, up_weight, True, jnp.bfloat16)
 
-    parts = jnp.stack([mixed_part, input_part])
-    summed = lax.psum_scatter(parts, "tensor", scatter_dimension=2, tiled=True)
+    parts = jnp.stack([mixed_part, input_part]).reshape(2, slot_count, shards, piece)
+    parts = jnp.transpose(parts, (2, 0, 1, 3))
+    summed = lax.psum_scatter(parts, "tensor", scatter_dimension=0, tiled=False)
     summed = summed.astype(jnp.float32).astype(jnp.bfloat16)
 
-    back = jnp.transpose(summed, (1, 0, 2)).reshape(groups, capacity, 2 * piece)
+    back = jnp.transpose(summed, (1, 0, 2)).reshape(groups, capacity * 2 * piece // BLOCK, BLOCK)
     returned = lax.all_to_all(back, "dp", split_axis=0, concat_axis=0, tiled=True)
     flattened = returned.reshape(slot_count, 2 * piece)
     results = jnp.dot(placer.T, flattened, preferred_element_type=jnp.float32).astype(jnp.bfloat16)

time: 195 us -> 201 us (1.031)
  blocking collectives: 71.1 us -> 75.5 us
  local copies, waits for them, and re-layouts: 9.96 us -> 14.2 us
  waiting for transfers between devices: 59 us -> 56.3 us
    unnamed x14 -> x16, local copies, waits for them, and re-layouts: 0.79 us -> 5.4 us
    all_to_all x1, blocking collectives: 38.9 us -> 43.3 us  [per_device(): lax.all_to_all(outgoing, 'dp', split_axis=0, concat_axis=0, tiled=True)]
    squeeze x1 -> x0, local copies, waits for them, and re-layouts: 2.72 us -> none  [per_device(): rows_in, grad_rows = (gathered[0], gathered[1])]
    all_gather x1, waiting for transfers between devices: 16.4 us -> 13.8 us  [per_device(): gathered = lax.all_gather(both, 'tensor', axis=0, tiled=False)]
    another operation x4 -> x3, other arithmetic: 3.17 us -> 0.72 us  [the longest x1 0.7 us: per_device(): both = jnp.stack([feats[:, :piece], feats[:, piece:]])]
  transfers between devices with their start and end apart: 2 -> 2, of which waited for: 2 -> 2; matrix products, arithmetic and copies ran while one was open for 4% -> 5% of each run, Pallas kernels for 0% -> 0%
where the time goes in v2:
time: 201 us
  blocking collectives  75.5 us (38%)
  waiting for transfers between devices  56.3 us (28%)
  Pallas kernels  27.9 us (14%)
  between operations  14.4 us (7%)
  local copies, waits for them, and re-layouts  14.2 us (7%)
  other arithmetic  9.37 us (5%)
  matrix products  2.73 us (1%)
    all_to_all x1, blocking collectives, per_device(): lax.all_to_all(outgoing, 'dp', split_axis=0, concat_axis=0, tiled=True)  43.3 us
    reduce_scatter x1, waiting for transfers between devices, per_device(): summed = lax.psum_scatter(parts, 'tensor', scatter_dimension=0, tiled=False)  42.4 us
    all_to_all x1, blocking collectives, per_device(): lax.all_to_all(back, 'dp', split_axis=0, concat_axis=0, tiled=True)  32.1 us
    pallas_call x4, Pallas kernels, masked_product(): pl.pallas_call(functools.partial(masked_kernel, per=per, turned=turned),...  27.9 us
    all_gather x1, waiting for transfers between devices, per_device(): gathered = lax.all_gather(both, 'tensor', axis=0, tiled=False)  13.8 us
    unnamed x16, local copies, waits for them, and re-layouts  5.4 us
  transfers between devices with their start and end apart: 2, of which 2 were waited for; matrix products, arithmetic and copies ran while one was open for 5% of the time, Pallas kernels for 0%

profile of v2, /device:TPU:7, one launch (start us, length us, event | category | flops | bytes accessed | tf_op | source)
XLA Modules:
  0.0 200.6 jit_solution(6866159447540799272)
XLA Ops:
  7.2 0.7 and_select_fusion
  8.6 1.1 convolution_convert_fusion.4
  10.3 43.3 %all_to_all.10 = bf16[96,16,128]{2,1,0:T(8,128)(2,1)S(1)} all-to-all(bf16[96,16,128]{2,1,0:T(8,128)(2,1)S(1)} %maximum_maximum_fusion), channel_id=1, replica_groups=mesh['dp'=96,'tensor'=8] {'dp'}, dimensions={0} | all-to-all | bytes 786432 | tf_op jit(solution)/shard_map/all_to_all | solution.py:93
  53.8 0.7 pad_maximum_fusion
  55.2 0.4 copy.45
  55.9 0.8 fusion.12.e_ref
  56.7 0.9 fusion.4.e_ref
  57.6 1.7 convert_reduce_fusion
  59.5 0.3 fusion.3
  59.8 0.9 copy.64
  60.6 0.3 fusion.2
  60.9 0.8 copy.65
  61.8 0.4 fusion
  62.2 1.1 copy.63
  63.3 0.4 fusion.1
  63.7 1.1 copy.62
  64.8 13.8 %all-gather.3.cloned.1.call-done = bf16[16,192,256]{2,1,0:T(8,128)(2,1)} async-done(((bf16[2,192,256]{2,1,0:T(8,128)(2,1)}), bf16[16,192,256]{2,1,0:T(8,128)(2,1)}) %all-gather.3.cloned.1.call-update) | async-done | bytes 1572880 | tf_op jit(solution)/shard_map/all_gather | solution.py:98
  78.6 1.5 fusion.30
  80.1 1.0 copy.54
  81.1 1.0 copy.50
  82.1 7.1 %shard_map.88 = f32[192,1024]{1,0:T(8,128)} custom-call(bf16[192,2048]{1,0:T(8,128)(2,1)} %bitcast.81, bf16[8,192,128]{2,1,0:T(8,128)(2,1)} %bitcast.92, bf16[128,2048]{1,0:T(8,128)(2,1)} %fusion.4.e_ref, bf16[1024,2048]{1,0:T(8,128)(2,1)} %bitcast.76), custom_call_target="tpu_custom_call" | custom-call | tf_op jit(solution)/shard_map/pallas_call | solution.py:56
  89.2 6.8 %shard_map.86 = f32[192,1024]{1,0:T(8,128)} custom-call(bf16[192,2048]{1,0:T(8,128)(2,1)} %bitcast.80, bf16[8,192,128]{2,1,0:T(8,128)(2,1)} %bitcast.93, bf16[128,2048]{1,0:T(8,128)(2,1)} %fusion.4.e_ref, bf16[2048,1024]{1,0:T(8,128)(2,1)} %w_ref.3), custom_call_target="tpu_custom_call" | custom-call | tf_op jit(solution)/shard_map/pallas_call | solution.py:56
  96.0 2.6 %multiply_convert_fusion = (bf16[192,1024]{1,0:T(8,128)(2,1)}, bf16[192,1024]{1,0:T(8,128)(2,1)}) fusion(f32[192,1024]{1,0:T(8,128)} %shard_map.86, f32[192,1024]{1,0:T(8,128)S(1)} %copy-done), kind=kLoop, calls=%fused_computation.24 | loop fusion | flops 4325376 | bytes 2359296 | tf_op jit(solution)/shard_map/convert_element_type | solution.py:111
  98.6 7.1 %shard_map.87 = bf16[192,2048]{1,0:T(8,128)(2,1)} custom-call(bf16[192,1024]{1,0:T(8,128)(2,1)} %get-tuple-element.4.x_ref, bf16[16,192,128]{2,1,0:T(8,128)(2,1)} %bitcast.79, bf16[128,1024]{1,0:T(8,128)(2,1)} %fusion.12.e_ref, bf16[1024,2048]{1,0:T(8,128)(2,1)} %bitcast.77), custom_call_target="tpu_custom_call" | custom-call | tf_op jit(solution)/shard_map/pallas_call | solution.py:56
  105.6 1.3 copy.53
  107.1 7.0 %shard_map.89 = bf16[192,2048]{1,0:T(8,128)(2,1)} custom-call(bf16[192,1024]{1,0:T(8,128)(2,1)} %get-tuple-element.5.x_ref, bf16[16,192,128]{2,1,0:T(8,128)(2,1)} %bitcast.78, bf16[128,1024]{1,0:T(8,128)(2,1)} %fusion.12.e_ref, bf16[2048,1024]{1,0:T(8,128)(2,1)} %w_ref.3), custom_call_target="tpu_custom_call" | custom-call | tf_op jit(solution)/shard_map/pallas_call | solution.py:56
  114.1 1.3 copy.55
  115.6 1.3 maximum_bitcast_fusion
  116.9 42.4 %reduce-scatter.2.cloned.1.call-done = bf16[1,2,192,256]{3,2,1,0:T(8,128)(2,1)} async-done(((bf16[8,2,192,256]{3,2,1,0:T(8,128)(2,1)}), bf16[1,2,192,256]{3,2,1,0:T(8,128)(2,1)}) %reduce-scatter.2.cloned.1.call-update) | async-done | bytes 196624 | tf_op jit(solution)/shard_map/reduce_scatter | solution.py:119
  159.3 1.1 copy.43
  160.6 32.1 %all_to_all.11 = bf16[96,8,128]{2,1,0:T(8,128)(2,1)S(1)} all-to-all(bf16[96,8,128]{2,1,0:T(8,128)(2,1)S(1)} %reshape.147), channel_id=1, replica_groups=mesh['dp'=96,'tensor'=8] {'dp'}, dimensions={0} | all-to-all | bytes 393216 | tf_op jit(solution)/shard_map/all_to_all | solution.py:123
  193.1 0.7 fusion.31
  (46 shorter events, 3.4 us)
Async XLA Ops:
  7.2 71.5 %all-gather.3.cloned.1.call-start = ((), (), s32[]{:S(2)}) async-start(), calls=%async_computation.4 | async-start | bytes 1769472 | tf_op jit(solution)/shard_map/all_gather | solution.py:98
  10.1 44.6 %copy-start.2 = (s32[100,8,16]{0,2,1:T(8,128)S(1)}, s32[100,8,16]{0,2,1:T(8,128)}, u32[]{:S(2)}) copy-start(s32[100,8,16]{0,2,1:T(8,128)} %param.11) | copy-start | bytes 153604
  10.3 44.5 %copy-start.1 = (s32[100,16,8]{0,2,1:T(8,128)S(1)}, s32[100,16,8]{0,2,1:T(8,128)}, u32[]{:S(2)}) copy-start(s32[100,16,8]{0,2,1:T(8,128)} %param.10) | copy-start | bytes 153604
  54.5 104.8 %reduce-scatter.2.cloned.1.call-start = ((), (), s32[]{:S(2)}) async-start(), calls=%async_computation.3 | async-start | bytes 1769472 | tf_op jit(solution)/shard_map/reduce_scatter | solution.py:119
  89.2 6.8 %copy-start = (f32[192,1024]{1,0:T(8,128)S(1)}, f32[192,1024]{1,0:T(8,128)}, u32[]{:S(2)}) copy-start(f32[192,1024]{1,0:T(8,128)} %shard_map.88) | copy-start | bytes 2359300
Sparse Core Ops, SparseCore 0:
  54.6 23.9 all-gather.2
  117.0 42.2 reduce-scatter.1

commit v3 on v2

--- a/solution.py
+++ b/solution.py
@@ -23,7 +23,7 @@
     return jnp.transpose(looked, (1, 0, 2)), blocks_in
 
 
-def masked_kernel(x_ref, m_ref, e_ref, w_ref, o_ref, *, per, turned):
+def masked_kernel(x_ref, m_ref, e_ref, w_ref, o_ref, *, per, turned, piece):
     x = x_ref[...]
     for b in range(per):
         spread = jnp.dot(m_ref[b], e_ref[...], preferred_element_type=jnp.float32).astype(x.dtype)
@@ -36,10 +36,14 @@
         else:
             w = w_ref[:, b * BLOCK:(b + 1) * BLOCK]
             acc = jnp.dot(masked, w, preferred_element_type=jnp.float32)
-        o_ref[:, b * BLOCK:(b + 1) * BLOCK] = acc.astype(o_ref.dtype)
+        if piece:
+            at = b * BLOCK
+            o_ref[at // piece, :, at % piece:at % piece + BLOCK] = acc.astype(o_ref.dtype)
+        else:
+            o_ref[:, b * BLOCK:(b + 1) * BLOCK] = acc.astype(o_ref.dtype)
 
 
-def masked_product(x, masks, blocks_in, weight, turned, out_dtype):
+def masked_product(x, masks, blocks_in, weight, turned, out_dtype, piece=0):
     rows, width = x.shape
     blocks_out = masks.shape[0]
     per = max(1, blocks_out // STEPS)
@@ -53,8 +57,14 @@
         w_spec = pl.BlockSpec((cols, width), lambda j: (j, 0))
     else:
         w_spec = pl.BlockSpec((width, cols), lambda j: (0, j))
+    if piece:
+        out_spec = pl.BlockSpec((cols // piece, rows, piece), lambda j: (j, 0, 0))
+        out_shape = (blocks_out * BLOCK // piece, rows, piece)
+    else:
+        out_spec = pl.BlockSpec((rows, cols), lambda j: (0, j))
+        out_shape = (rows, blocks_out * BLOCK)
     return pl.pallas_call(
-        functools.partial(masked_kernel, per=per, turned=turned),
+        functools.partial(masked_kernel, per=per, turned=turned, piece=piece),
         grid=(steps,),
         in_specs=[
             pl.BlockSpec((rows, width), lambda j: (0, 0)),
@@ -62,9 +72,14 @@
             pl.BlockSpec((BLOCK, width), lambda j: (0, 0)),
             w_spec,
         ],
-        out_specs=pl.BlockSpec((rows, cols), lambda j: (0, j)),
-        out_shape=jax.ShapeDtypeStruct((rows, blocks_out * BLOCK), out_dtype),
+        out_specs=out_spec,
+        out_shape=jax.ShapeDtypeStruct(out_shape, out_dtype),
     )(x, masks, expand, weight)
+
+
+def settle(part):
+    arrived = lax.all_to_all(part, "tensor", split_axis=0, concat_axis=0, tiled=True)
+    return jnp.sum(arrived.astype(jnp.float32), axis=0).astype(jnp.bfloat16)
 
 
 def per_device(tokens, cotangent, pair_ids, up_mask, down_mask, up_weight, down_weight):
@@ -109,15 +124,14 @@
     before_act = masked_product(rows_in, up_fwd, up_in, up_weight, False, jnp.float32)
     activated, backward_function = jax.vjp(jax.nn.gelu, before_act)
     hidden = activated.astype(jnp.bfloat16)
-    mixed_part = masked_product(hidden, down_fwd, down_in, down_local, False, jnp.bfloat16)
+    mixed_part = masked_product(hidden, down_fwd, down_in, down_local, False, jnp.bfloat16, piece)
+    mixed_sum = settle(mixed_part)
     grad_hidden = masked_product(grad_rows, down_bwd, down_out, down_local, True, jnp.float32)
     grad_pre = backward_function(grad_hidden)[0].astype(jnp.bfloat16)
-    input_part = masked_product(grad_pre, up_bwd, up_out, up_weight, True, jnp.bfloat16)
+    input_part = masked_product(grad_pre, up_bwd, up_out, up_weight, True, jnp.bfloat16, piece)
+    input_sum = settle(input_part)
 
-    parts = jnp.stack([mixed_part, input_part]).reshape(2, slot_count, shards, piece)
-    parts = jnp.transpose(parts, (2, 0, 1, 3))
-    summed = lax.psum_scatter(parts, "tensor", scatter_dimension=0, tiled=False)
-    summed = summed.astype(jnp.float32).astype(jnp.bfloat16)
+    summed = jnp.stack([mixed_sum, input_sum])
 
     back = jnp.transpose(summed, (1, 0, 2)).reshape(groups, capacity * 2 * piece // BLOCK, BLOCK)
     returned = lax.all_to_all(back, "dp", split_axis=0, concat_axis=0, tiled=True)

time: 201 us -> 182 us (0.905)
  the two profiles are of different devices: /device:TPU:7 before, /device:TPU:8 now
where the time goes in v3:
time: 182 us; the launch traced here: 181 us
  blocking collectives  78.2 us (43%)
  waiting for transfers between devices  32.3 us (18%)
  Pallas kernels  27.7 us (15%)
  between operations  14.4 us (8%)
  local copies, waits for them, and re-layouts  10.3 us (6%)
  other arithmetic  8.32 us (5%)
  starting transfers between devices  7.31 us (4%)
  matrix products  2.73 us (2%)
    all_to_all x1, blocking collectives, per_device(): lax.all_to_all(outgoing, 'dp', split_axis=0, concat_axis=0, tiled=True)  44.8 us
    all_to_all x1, blocking collectives, per_device(): lax.all_to_all(back, 'dp', split_axis=0, concat_axis=0, tiled=True)  33.3 us
    pallas_call x4, Pallas kernels, masked_product(): pl.pallas_call(functools.partial(masked_kernel, per=per, turned=turned, p...  27.7 us
    all_to_all x2, waiting for transfers between devices, settle(): lax.all_to_all(part, 'tensor', split_axis=0, concat_axis=0, tiled=True)  17.3 us
    all_gather x1, waiting for transfers between devices, per_device(): gathered = lax.all_gather(both, 'tensor', axis=0, tiled=False)  15 us
    all_to_all x2, starting transfers between devices, settle(): lax.all_to_all(part, 'tensor', split_axis=0, concat_axis=0, tiled=True)  7.27 us
    reshape x4, local copies, waits for them, and re-layouts, picked_masks(): looked = looked.reshape(pairs_here.shape[0], blocks_out, BLOCK)  3.81 us
  transfers between devices with their start and end apart: 3, of which 3 were waited for; matrix products, arithmetic and copies ran while one was open for 5% of the time, Pallas kernels for 4%

profile of v3, /device:TPU:8, one launch (start us, length us, event | category | flops | bytes accessed | tf_op | source)
XLA Modules:
  0.0 181.2 jit_solution(9370836719067291698)
XLA Ops:
  7.2 0.7 and_select_fusion
  8.6 1.1 convolution_convert_fusion.4
  10.3 44.8 %all_to_all.20 = bf16[96,16,128]{2,1,0:T(8,128)(2,1)S(1)} all-to-all(bf16[96,16,128]{2,1,0:T(8,128)(2,1)S(1)} %maximum_maximum_fusion), channel_id=1, replica_groups=mesh['dp'=96,'tensor'=8] {'dp'}, dimensions={0} | all-to-all | bytes 786432 | tf_op jit(solution)/shard_map/all_to_all | solution.py:108
  55.3 0.7 pad_maximum_fusion
  56.4 0.4 copy.49
  57.1 0.8 fusion.12.e_ref
  57.9 0.9 fusion.4.e_ref
  58.8 1.7 convert_reduce_fusion
  60.6 0.3 fusion.3
  60.9 0.8 copy.66
  61.7 0.3 fusion.2
  62.0 0.8 copy.67
  62.8 0.4 fusion
  63.3 1.1 copy.65
  64.4 15.0 %all-gather.3.cloned.1.call-done = bf16[16,192,256]{2,1,0:T(8,128)(2,1)} async-done(((bf16[2,192,256]{2,1,0:T(8,128)(2,1)}), bf16[16,192,256]{2,1,0:T(8,128)(2,1)}) %all-gather.3.cloned.1.call-update) | async-done | bytes 1572880 | tf_op jit(solution)/shard_map/all_gather | solution.py:113
  79.3 1.5 fusion.30
  80.9 1.0 copy.57
  81.9 1.0 copy.54
  82.8 7.0 %shard_map.88 = f32[192,1024]{1,0:T(8,128)} custom-call(bf16[192,2048]{1,0:T(8,128)(2,1)} %bitcast.73, bf16[8,192,128]{2,1,0:T(8,128)(2,1)} %bitcast.81, bf16[128,2048]{1,0:T(8,128)(2,1)} %fusion.4.e_ref, bf16[1024,2048]{1,0:T(8,128)(2,1)} %bitcast.69), custom_call_target="tpu_custom_call" | custom-call | tf_op jit(solution)/shard_map/pallas_call | solution.py:66
  89.8 6.8 %shard_map.86 = f32[192,1024]{1,0:T(8,128)} custom-call(bf16[192,2048]{1,0:T(8,128)(2,1)} %bitcast.72, bf16[8,192,128]{2,1,0:T(8,128)(2,1)} %bitcast.82, bf16[128,2048]{1,0:T(8,128)(2,1)} %fusion.4.e_ref, bf16[2048,1024]{1,0:T(8,128)(2,1)} %w_ref.3), custom_call_target="tpu_custom_call" | custom-call | tf_op jit(solution)/shard_map/pallas_call | solution.py:66
  96.6 2.6 %multiply_convert_fusion = (bf16[192,1024]{1,0:T(8,128)(2,1)}, bf16[192,1024]{1,0:T(8,128)(2,1)}) fusion(f32[192,1024]{1,0:T(8,128)} %shard_map.86, f32[192,1024]{1,0:T(8,128)S(1)} %copy-done), kind=kLoop, calls=%fused_computation.23 | loop fusion | flops 4325376 | bytes 2359296 | tf_op jit(solution)/shard_map/convert_element_type | solution.py:126
  99.2 7.0 %shard_map.87 = bf16[8,192,256]{2,1,0:T(8,128)(2,1)} custom-call(bf16[192,1024]{1,0:T(8,128)(2,1)} %get-tuple-element.4.x_ref, bf16[16,192,128]{2,1,0:T(8,128)(2,1)} %bitcast.71, bf16[128,1024]{1,0:T(8,128)(2,1)} %fusion.12.e_ref, bf16[1024,2048]{1,0:T(8,128)(2,1)} %bitcast.70), custom_call_target="tpu_custom_call" | custom-call | tf_op jit(solution)/shard_map/pallas_call | solution.py:66
  106.3 3.5 %all-to-all-start.1 = ((bf16[8,192,256]{2,1,0:T(8,128)(2,1)}), bf16[8,192,256]{2,1,0:T(8,128)(2,1)S(1)}, u32[]{:S(2)}, u32[]{:S(2)}) async-start(bf16[8,192,256]{2,1,0:T(8,128)(2,1)} %shard_map.87), calls=%async_computation.1 | async-start | bytes 1572864 | tf_op jit(solution)/shard_map/all_to_all | solution.py:81
  109.9 0.4 fusion.1
  110.3 1.1 copy.64
  111.4 6.9 %shard_map.89 = bf16[8,192,256]{2,1,0:T(8,128)(2,1)} custom-call(bf16[192,1024]{1,0:T(8,128)(2,1)} %get-tuple-element.5.x_ref, bf16[16,192,128]{2,1,0:T(8,128)(2,1)} %bitcast.74, bf16[128,1024]{1,0:T(8,128)(2,1)} %fusion.12.e_ref, bf16[2048,1024]{1,0:T(8,128)(2,1)} %w_ref.3), custom_call_target="tpu_custom_call" | custom-call | tf_op jit(solution)/shard_map/pallas_call | solution.py:66
  118.3 4.5 %all-to-all-done.1 = bf16[8,192,256]{2,1,0:T(8,128)(2,1)S(1)} async-done(((bf16[8,192,256]{2,1,0:T(8,128)(2,1)}), bf16[8,192,256]{2,1,0:T(8,128)(2,1)S(1)}, u32[]{:S(2)}, u32[]{:S(2)}) %all-to-all-start.1) | async-done | bytes 786464 | tf_op jit(solution)/shard_map/all_to_all | solution.py:81
  122.9 3.7 %all-to-all-start.2 = ((bf16[8,192,256]{2,1,0:T(8,128)(2,1)}), bf16[8,192,256]{2,1,0:T(8,128)(2,1)S(1)}, u32[]{:S(2)}, u32[]{:S(2)}) async-start(bf16[8,192,256]{2,1,0:T(8,128)(2,1)} %shard_map.89), calls=%async_computation.2 | async-start | bytes 1572864 | tf_op jit(solution)/shard_map/all_to_all | solution.py:81
  126.7 12.7 %all-to-all-done.2 = bf16[8,192,256]{2,1,0:T(8,128)(2,1)S(1)} async-done(((bf16[8,192,256]{2,1,0:T(8,128)(2,1)}), bf16[8,192,256]{2,1,0:T(8,128)(2,1)S(1)}, u32[]{:S(2)}, u32[]{:S(2)}) %all-to-all-start.2) | async-done | bytes 786464 | tf_op jit(solution)/shard_map/all_to_all | solution.py:81
  139.9 33.3 %all_to_all.21 = bf16[96,8,128]{2,1,0:T(8,128)(2,1)S(1)} all-to-all(bf16[96,8,128]{2,1,0:T(8,128)(2,1)S(1)} %reshape.142), channel_id=1, replica_groups=mesh['dp'=96,'tensor'=8] {'dp'}, dimensions={0} | all-to-all | bytes 393216 | tf_op jit(solution)/shard_map/all_to_all | solution.py:137
  173.4 0.2 convolution_convert_fusion.5
  173.6 0.7 fusion.31
  (45 shorter events, 3.0 us)
Async XLA Ops:
  7.2 72.2 %all-gather.3.cloned.1.call-start = ((), (), s32[]{:S(2)}) async-start(), calls=%async_computation.4 | async-start | bytes 1769472 | tf_op jit(solution)/shard_map/all_gather | solution.py:113
  10.1 45.9 %copy-start.1 = (s32[100,8,16]{0,2,1:T(8,128)S(1)}, s32[100,8,16]{0,2,1:T(8,128)}, u32[]{:S(2)}) copy-start(s32[100,8,16]{0,2,1:T(8,128)} %param.11) | copy-start | bytes 153604
  10.3 45.8 %copy-start.2 = (s32[100,16,8]{0,2,1:T(8,128)S(1)}, s32[100,16,8]{0,2,1:T(8,128)}, u32[]{:S(2)}) copy-start(s32[100,16,8]{0,2,1:T(8,128)} %param.10) | copy-start | bytes 153604
  89.8 6.8 %copy-start = (f32[192,1024]{1,0:T(8,128)S(1)}, f32[192,1024]{1,0:T(8,128)}, u32[]{:S(2)}) copy-start(f32[192,1024]{1,0:T(8,128)} %shard_map.88) | copy-start | bytes 2359300
  106.3 16.6 %all-to-all-start.1 = ((bf16[8,192,256]{2,1,0:T(8,128)(2,1)}), bf16[8,192,256]{2,1,0:T(8,128)(2,1)S(1)}, u32[]{:S(2)}, u32[]{:S(2)}) async-start(bf16[8,192,256]{2,1,0:T(8,128)(2,1)} %shard_map.87), calls=%async_computation.1 | async-start | bytes 1572864 | tf_op jit(solution)/shard_map/all_to_all | solution.py:81
  122.9 16.6 %all-to-all-start.2 = ((bf16[8,192,256]{2,1,0:T(8,128)(2,1)}), bf16[8,192,256]{2,1,0:T(8,128)(2,1)S(1)}, u32[]{:S(2)}, u32[]{:S(2)}) async-start(bf16[8,192,256]{2,1,0:T(8,128)(2,1)} %shard_map.89), calls=%async_computation.2 | async-start | bytes 1572864 | tf_op jit(solution)/shard_map/all_to_all | solution.py:81
Sparse Core Ops, SparseCore 0:
  56.1 23.1 all-gather.2

commit v4 on v3

--- a/solution.py
+++ b/solution.py
@@ -95,25 +95,39 @@
     placer = placing.astype(jnp.bfloat16)
     slot_pairs = jnp.sum(jnp.where(placing, pair_ids[None, :] + 1, 0), axis=1) - 1
 
-    payload = jnp.concatenate([tokens, cotangent], axis=1)
-    outgoing = jnp.dot(placer, payload, preferred_element_type=jnp.float32).astype(jnp.bfloat16)
-    feat_rows = outgoing.reshape(groups, capacity * 2 * piece // BLOCK, BLOCK)
+    def route(values, extra):
+        moved = jnp.dot(placer, values, preferred_element_type=jnp.float32).astype(jnp.bfloat16)
+        rows = [moved.reshape(groups, capacity * piece // BLOCK, BLOCK)] + extra
+        used = sum(r.shape[1] for r in rows)
+        tile_rows = -(-used // 8) * 8
+        if tile_rows > used:
+            rows.append(jnp.zeros((groups, tile_rows - used, BLOCK), jnp.bfloat16))
+        arrived = lax.all_to_all(
+            jnp.concatenate(rows, axis=1), "dp", split_axis=0, concat_axis=0, tiled=True
+        )
+        return arrived, capacity * piece // BLOCK
+
+    def widen(arrived, feat_rows):
+        part = arrived[:, :feat_rows, :].reshape(slot_count, piece)
+        gathered = lax.all_gather(part, "tensor", axis=0, tiled=False)
+        shards = gathered.shape[0]
+        return jnp.transpose(gathered, (1, 0, 2)).reshape(slot_count, shards * piece)
+
     pair_rows = jnp.broadcast_to(
         slot_pairs.astype(jnp.bfloat16).reshape(groups, capacity, 1), (groups, capacity, BLOCK)
     )
-    used = feat_rows.shape[1] + capacity
-    tile_rows = -(-used // 16) * 16
-    filler = jnp.zeros((groups, tile_rows - used, BLOCK), jnp.bfloat16)
-    outgoing = jnp.concatenate([feat_rows, pair_rows, filler], axis=1)
-    arrived = lax.all_to_all(outgoing, "dp", split_axis=0, concat_axis=0, tiled=True)
-    feats = arrived[:, :feat_rows.shape[1], :].reshape(slot_count, 2 * piece)
-    pairs_here = arrived[:, feat_rows.shape[1]:used, 0].reshape(slot_count).astype(jnp.int32)
+    arrived_tok, feat_rows = route(tokens, [pair_rows])
+    pairs_here = arrived_tok[:, feat_rows:feat_rows + capacity, 0].reshape(slot_count).astype(jnp.int32)
+    rows_in = widen(arrived_tok, feat_rows)
+    arrived_cot, _ = route(cotangent, [])
+    grad_rows = widen(arrived_cot, feat_rows)
 
-    both = jnp.stack([feats[:, :piece], feats[:, piece:]])
-    gathered = lax.all_gather(both, "tensor", axis=0, tiled=False)
-    shards = gathered.shape[0]
-    gathered = jnp.transpose(gathered, (1, 2, 0, 3)).reshape(2, slot_count, shards * piece)
-    rows_in, grad_rows = gathered[0], gathered[1]
+    def send_back(values):
+        returned = lax.all_to_all(
+            values.reshape(groups, capacity * piece // BLOCK, BLOCK), "dp", split_axis=0, concat_axis=0, tiled=True
+        )
+        flattened = returned.reshape(slot_count, piece)
+        return jnp.dot(placer.T, flattened, preferred_element_type=jnp.float32).astype(jnp.bfloat16)
 
     up_fwd, up_in = picked_masks(up_mask, pairs_here, (0, 2, 1))
     up_bwd, up_out = picked_masks(up_mask, pairs_here, (0, 1, 2))
@@ -126,18 +140,13 @@
     hidden = activated.astype(jnp.bfloat16)
     mixed_part = masked_product(hidden, down_fwd, down_in, down_local, False, jnp.bfloat16, piece)
     mixed_sum = settle(mixed_part)
+    mixed = send_back(mixed_sum)
     grad_hidden = masked_product(grad_rows, down_bwd, down_out, down_local, True, jnp.float32)
     grad_pre = backward_function(grad_hidden)[0].astype(jnp.bfloat16)
     input_part = masked_product(grad_pre, up_bwd, up_out, up_weight, True, jnp.bfloat16, piece)
     input_sum = settle(input_part)
 
-    summed = jnp.stack([mixed_sum, input_sum])
-
-    back = jnp.transpose(summed, (1, 0, 2)).reshape(groups, capacity * 2 * piece // BLOCK, BLOCK)
-    returned = lax.all_to_all(back, "dp", split_axis=0, concat_axis=0, tiled=True)
-    flattened = returned.reshape(slot_count, 2 * piece)
-    results = jnp.dot(placer.T, flattened, preferred_element_type=jnp.float32).astype(jnp.bfloat16)
-    return (results[:, :piece], results[:, piece:])
+    return (mixed, send_back(input_sum))
 
 
 def solution(mesh):

time: 182 us -> 193 us (1.060)
  blocking collectives: 78.2 us -> 27.3 us
  starting transfers between devices: 7.31 us -> 57.1 us
  waiting for transfers between devices: 32.3 us -> 54.3 us
  between operations: 14.4 us -> 0.91 us
  other arithmetic: 8.32 us -> 10.8 us
    all_to_all x2 -> x0, blocking collectives: 78.2 us -> none  [the longest x1 44.8 us: per_device(): lax.all_to_all(outgoing, 'dp', split_axis=0, concat_axis=0, tiled=True)]
    all_to_all x0 -> x4, starting transfers between devices: none -> 49.9 us  [the longest x2 28 us: route(): lax.all_to_all(jnp.concatenate(rows, axis=1), 'dp', split_axis=0, concat_...]
    all_to_all x0 -> x4, waiting for transfers between devices: none -> 37.4 us  [the longest x2 27.1 us: send_back(): lax.all_to_all(values.reshape(groups, capacity * piece // BLOCK, BLOCK),...]
    all_gather x0 -> x2, blocking collectives: none -> 27.3 us  [widen(): gathered = lax.all_gather(part, 'tensor', axis=0, tiled=False)]
    all_gather x1 -> x0, waiting for transfers between devices: 15 us -> none  [per_device(): gathered = lax.all_gather(both, 'tensor', axis=0, tiled=False)]
    reshape x4 -> x8, local copies, waits for them, and re-layouts: 0.51 us -> 3.49 us  [the longest x2 1.98 us: widen(): jnp.transpose(gathered, (1, 0, 2)).reshape(slot_count, shards * piece)]
    slice x3 -> x2, local copies, waits for them, and re-layouts: 2.18 us -> 0.06 us  [widen(): part = arrived[:, :feat_rows, :].reshape(slot_count, piece)]
    unnamed x14 -> x12, local copies, waits for them, and re-layouts: 2.75 us -> 0.79 us
  transfers between devices with their start and end apart: 3 -> 6, of which waited for: 3 -> 5; matrix products, arithmetic and copies ran while one was open for 5% -> 8% of each run, Pallas kernels for 4% -> 4%
where the time goes in v4:
time: 193 us; the launch traced here: 192 us
  starting transfers between devices  57.1 us (30%)
  waiting for transfers between devices  54.3 us (28%)
  Pallas kernels  27.8 us (14%)
  blocking collectives  27.3 us (14%)
  other arithmetic  10.8 us (6%)
  local copies, waits for them, and re-layouts  9.8 us (5%)
  matrix products  4.3 us (2%)
    all_to_all x2, starting transfers between devices, route(): lax.all_to_all(jnp.concatenate(rows, axis=1), 'dp', split_axis=0, concat_...  28 us
    pallas_call x4, Pallas kernels, masked_product(): pl.pallas_call(functools.partial(masked_kernel, per=per, turned=turned, p...  27.8 us
    all_gather x2, blocking collectives, widen(): gathered = lax.all_gather(part, 'tensor', axis=0, tiled=False)  27.3 us
    all_to_all x2, waiting for transfers between devices, send_back(): lax.all_to_all(values.reshape(groups, capacity * piece // BLOCK, BLOCK),...  27.1 us
    all_to_all x2, starting transfers between devices, send_back(): lax.all_to_all(values.reshape(groups, capacity * piece // BLOCK, BLOCK),...  21.8 us
    all_to_all x2, waiting for transfers between devices, settle(): lax.all_to_all(part, 'tensor', split_axis=0, concat_axis=0, tiled=True)  16.9 us
    all_to_all x2, waiting for transfers between devices, route(): lax.all_to_all(jnp.concatenate(rows, axis=1), 'dp', split_axis=0, concat_...  10.4 us
    all_to_all x2, starting transfers between devices, settle(): lax.all_to_all(part, 'tensor', split_axis=0, concat_axis=0, tiled=True)  7.24 us
  transfers between devices with their start and end apart: 6, of which 5 were waited for; matrix products, arithmetic and copies ran while one was open for 8% of the time, Pallas kernels for 4%

profile of v4, /device:TPU:8, one launch (start us, length us, event | category | flops | bytes accessed | tf_op | source)
XLA Modules:
  0.0 192.3 jit_solution(3334467245910260292)
XLA Ops:
  3.4 21.8 %all-to-all-start = ((bf16[96,8,128]{2,1,0:T(8,128)(2,1)}), bf16[96,8,128]{2,1,0:T(8,128)(2,1)S(1)}, u32[]{:S(2)}, u32[]{:S(2)}) async-start(bf16[96,8,128]{2,1,0:T(8,128)(2,1)} %maximum_maximum_fusion), calls=%async_computation | async-start | bytes 393216 | tf_op jit(solution)/shard_map/all_to_all | solution.py:105
  25.1 0.8 convert_bitcast_fusion.1
  26.0 1.0 convolution_convert_fusion.4
  27.8 0.8 convert_bitcast_fusion
  28.6 0.8 convert.18
  31.2 0.9 fusion.4.e_ref
  32.1 10.4 %all-to-all-done = bf16[96,8,128]{2,1,0:T(8,128)(2,1)S(1)} async-done(((bf16[96,8,128]{2,1,0:T(8,128)(2,1)}), bf16[96,8,128]{2,1,0:T(8,128)(2,1)S(1)}, u32[]{:S(2)}, u32[]{:S(2)}) %all-to-all-start) | async-done | bytes 196640 | tf_op jit(solution)/shard_map/all_to_all | solution.py:105
  42.4 6.3 %all-to-all-start.3 = ((bf16[96,8,128]{2,1,0:T(8,128)(2,1)}), bf16[96,8,128]{2,1,0:T(8,128)(2,1)S(1)}, u32[]{:S(2)}, u32[]{:S(2)}) async-start(bf16[96,8,128]{2,1,0:T(8,128)(2,1)} %concatenate.7), calls=%async_computation.3 | async-start | bytes 393216 | tf_op jit(solution)/shard_map/all_to_all | solution.py:105
  48.7 1.7 convert_reduce_fusion
  50.9 0.8 copy.52
  51.8 13.8 %all_gather.6 = bf16[8,192,256]{2,1,0:T(8,128)(2,1)S(1)} all-gather(bf16[1,192,256]{2,1,0:T(8,128)(2,1)S(1)} %all_gather_reshape.6), channel_id=1, replica_groups=mesh['dp'=96,'tensor'=8] {'tensor'}, dimensions={0}, use_global_device_ids=true | all-gather | bytes 884736 | tf_op jit(solution)/shard_map/all_gather | solution.py:112
  65.6 1.0 copy.41
  66.8 0.8 copy.51
  67.8 13.6 %all_gather.7 = bf16[8,192,256]{2,1,0:T(8,128)(2,1)S(1)} all-gather(bf16[1,192,256]{2,1,0:T(8,128)(2,1)S(1)} %all_gather_reshape.7), channel_id=1, replica_groups=mesh['dp'=96,'tensor'=8] {'tensor'}, dimensions={0}, use_global_device_ids=true | all-gather | bytes 884736 | tf_op jit(solution)/shard_map/all_gather | solution.py:112
  81.3 1.0 copy.42
  82.8 1.1 copy.50
  83.8 6.7 %shard_map.86 = f32[192,1024]{1,0:T(8,128)} custom-call(bf16[192,2048]{1,0:T(8,128)(2,1)} %bitcast.61, bf16[8,192,128]{2,1,0:T(8,128)(2,1)} %bitcast.70, bf16[128,2048]{1,0:T(8,128)(2,1)} %fusion.4.e_ref, bf16[2048,1024]{1,0:T(8,128)(2,1)} %w_ref.3), custom_call_target="tpu_custom_call" | custom-call | tf_op jit(solution)/shard_map/pallas_call | solution.py:66
  90.6 7.1 %shard_map.88 = f32[192,1024]{1,0:T(8,128)} custom-call(bf16[192,2048]{1,0:T(8,128)(2,1)} %bitcast.63, bf16[8,192,128]{2,1,0:T(8,128)(2,1)} %bitcast.71, bf16[128,2048]{1,0:T(8,128)(2,1)} %fusion.4.e_ref, bf16[1024,2048]{1,0:T(8,128)(2,1)} %bitcast.59), custom_call_target="tpu_custom_call" | custom-call | tf_op jit(solution)/shard_map/pallas_call | solution.py:66
  97.6 2.6 %fusion.11 = (bf16[192,1024]{1,0:T(8,128)(2,1)}, bf16[192,1024]{1,0:T(8,128)(2,1)}) fusion(f32[192,1024]{1,0:T(8,128)S(1)} %copy-done.1, f32[192,1024]{1,0:T(8,128)} %shard_map.88), kind=kLoop, calls=%fused_computation.22 | loop fusion | flops 4325376 | bytes 2359296 | tf_op jit(solution)/shard_map/convert_element_type | solution.py:145
  100.2 7.1 %shard_map.87 = bf16[8,192,256]{2,1,0:T(8,128)(2,1)} custom-call(bf16[192,1024]{1,0:T(8,128)(2,1)} %get-tuple-element.3.x_ref, bf16[16,192,128]{2,1,0:T(8,128)(2,1)} %bitcast.62, bf16[128,1024]{1,0:T(8,128)(2,1)} %fusion.12.e_ref, bf16[1024,2048]{1,0:T(8,128)(2,1)} %bitcast.60), custom_call_target="tpu_custom_call" | custom-call | tf_op jit(solution)/shard_map/pallas_call | solution.py:66
  107.3 3.7 %all-to-all-start.1 = ((bf16[8,192,256]{2,1,0:T(8,128)(2,1)}), bf16[8,192,256]{2,1,0:T(8,128)(2,1)S(1)}, u32[]{:S(2)}, u32[]{:S(2)}) async-start(bf16[8,192,256]{2,1,0:T(8,128)(2,1)} %shard_map.87), calls=%async_computation.1 | async-start | bytes 1572864 | tf_op jit(solution)/shard_map/all_to_all | solution.py:81
  111.6 1.1 copy.49
  112.7 6.9 %shard_map.89 = bf16[8,192,256]{2,1,0:T(8,128)(2,1)} custom-call(bf16[192,1024]{1,0:T(8,128)(2,1)} %get-tuple-element.2.x_ref, bf16[16,192,128]{2,1,0:T(8,128)(2,1)} %bitcast.64, bf16[128,1024]{1,0:T(8,128)(2,1)} %fusion.12.e_ref, bf16[2048,1024]{1,0:T(8,128)(2,1)} %w_ref.3), custom_call_target="tpu_custom_call" | custom-call | tf_op jit(solution)/shard_map/pallas_call | solution.py:66
  119.5 4.6 %all-to-all-done.1 = bf16[8,192,256]{2,1,0:T(8,128)(2,1)S(1)} async-done(((bf16[8,192,256]{2,1,0:T(8,128)(2,1)}), bf16[8,192,256]{2,1,0:T(8,128)(2,1)S(1)}, u32[]{:S(2)}, u32[]{:S(2)}) %all-to-all-start.1) | async-done | bytes 786464 | tf_op jit(solution)/shard_map/all_to_all | solution.py:81
  124.1 3.5 %all-to-all-start.4 = ((bf16[8,192,256]{2,1,0:T(8,128)(2,1)}), bf16[8,192,256]{2,1,0:T(8,128)(2,1)S(1)}, u32[]{:S(2)}, u32[]{:S(2)}) async-start(bf16[8,192,256]{2,1,0:T(8,128)(2,1)} %shard_map.89), calls=%async_computation.4 | async-start | bytes 1572864 | tf_op jit(solution)/shard_map/all_to_all | solution.py:81
  128.5 12.3 %all-to-all-done.4 = bf16[8,192,256]{2,1,0:T(8,128)(2,1)S(1)} async-done(((bf16[8,192,256]{2,1,0:T(8,128)(2,1)}), bf16[8,192,256]{2,1,0:T(8,128)(2,1)S(1)}, u32[]{:S(2)}, u32[]{:S(2)}) %all-to-all-start.4) | async-done | bytes 786464 | tf_op jit(solution)/shard_map/all_to_all | solution.py:81
  140.7 15.7 %all-to-all-start.2 = ((bf16[96,4,128]{2,1,0:T(4,128)(2,1)}), bf16[96,4,128]{2,1,0:T(4,128)(2,1)S(1)}, u32[]{:S(2)}, u32[]{:S(2)}) async-start(bf16[96,4,128]{2,1,0:T(4,128)(2,1)} %reshape.147), calls=%async_computation.2 | async-start | bytes 196608 | tf_op jit(solution)/shard_map/all_to_all | solution.py:126
  157.3 13.6 %all-to-all-done.2 = bf16[96,4,128]{2,1,0:T(4,128)(2,1)S(1)} async-done(((bf16[96,4,128]{2,1,0:T(4,128)(2,1)}), bf16[96,4,128]{2,1,0:T(4,128)(2,1)S(1)}, u32[]{:S(2)}, u32[]{:S(2)}) %all-to-all-start.2) | async-done | bytes 98336 | tf_op jit(solution)/shard_map/all_to_all | solution.py:126
  170.9 6.1 %all-to-all-start.5 = ((bf16[96,4,128]{2,1,0:T(4,128)(2,1)}), bf16[96,4,128]{2,1,0:T(4,128)(2,1)S(1)}, u32[]{:S(2)}, u32[]{:S(2)}) async-start(bf16[96,4,128]{2,1,0:T(4,128)(2,1)} %reshape.153), calls=%async_computation.5 | async-start | bytes 196608 | tf_op jit(solution)/shard_map/all_to_all | solution.py:126
  177.0 0.9 convolution_convert_fusion.7
  177.9 13.5 %all-to-all-done.5 = bf16[96,4,128]{2,1,0:T(4,128)(2,1)S(1)} async-done(((bf16[96,4,128]{2,1,0:T(4,128)(2,1)}), bf16[96,4,128]{2,1,0:T(4,128)(2,1)S(1)}, u32[]{:S(2)}, u32[]{:S(2)}) %all-to-all-start.5) | async-done | bytes 98336 | tf_op jit(solution)/shard_map/all_to_all | solution.py:126
  191.4 0.9 convolution_convert_fusion.6
  (52 shorter events, 8.7 us)
Async XLA Ops:
  0.6 1.5 copy-start
  3.4 39.1 %all-to-all-start = ((bf16[96,8,128]{2,1,0:T(8,128)(2,1)}), bf16[96,8,128]{2,1,0:T(8,128)(2,1)S(1)}, u32[]{:S(2)}, u32[]{:S(2)}) async-start(bf16[96,8,128]{2,1,0:T(8,128)(2,1)} %maximum_maximum_fusion), calls=%async_computation | async-start | bytes 393216 | tf_op jit(solution)/shard_map/all_to_all | solution.py:105
  42.4 25.2 %all-to-all-start.3 = ((bf16[96,8,128]{2,1,0:T(8,128)(2,1)}), bf16[96,8,128]{2,1,0:T(8,128)(2,1)S(1)}, u32[]{:S(2)}, u32[]{:S(2)}) async-start(bf16[96,8,128]{2,1,0:T(8,128)(2,1)} %concatenate.7), calls=%async_computation.3 | async-start | bytes 393216 | tf_op jit(solution)/shard_map/all_to_all | solution.py:105
  90.6 7.1 %copy-start.1 = (f32[192,1024]{1,0:T(8,128)S(1)}, f32[192,1024]{1,0:T(8,128)}, u32[]{:S(2)}) copy-start(f32[192,1024]{1,0:T(8,128)} %shard_map.86) | copy-start | bytes 2359300
  100.2 10.8 %copy-start.2 = (s32[100,16,8]{0,2,1:T(8,128)S(1)}, s32[100,16,8]{0,2,1:T(8,128)}, u32[]{:S(2)}) copy-start(s32[100,16,8]{0,2,1:T(8,128)} %param.10) | copy-start | bytes 153604
  107.3 16.8 %all-to-all-start.1 = ((bf16[8,192,256]{2,1,0:T(8,128)(2,1)}), bf16[8,192,256]{2,1,0:T(8,128)(2,1)S(1)}, u32[]{:S(2)}, u32[]{:S(2)}) async-start(bf16[8,192,256]{2,1,0:T(8,128)(2,1)} %shard_map.87), calls=%async_computation.1 | async-start | bytes 1572864 | tf_op jit(solution)/shard_map/all_to_all | solution.py:81
  124.1 16.6 %all-to-all-start.4 = ((bf16[8,192,256]{2,1,0:T(8,128)(2,1)}), bf16[8,192,256]{2,1,0:T(8,128)(2,1)S(1)}, u32[]{:S(2)}, u32[]{:S(2)}) async-start(bf16[8,192,256]{2,1,0:T(8,128)(2,1)} %shard_map.89), calls=%async_computation.4 | async-start | bytes 1572864 | tf_op jit(solution)/shard_map/all_to_all | solution.py:81
  140.7 30.1 %all-to-all-start.2 = ((bf16[96,4,128]{2,1,0:T(4,128)(2,1)}), bf16[96,4,128]{2,1,0:T(4,128)(2,1)S(1)}, u32[]{:S(2)}, u32[]{:S(2)}) async-start(bf16[96,4,128]{2,1,0:T(4,128)(2,1)} %reshape.147), calls=%async_computation.2 | async-start | bytes 196608 | tf_op jit(solution)/shard_map/all_to_all | solution.py:126
  170.9 20.5 %all-to-all-start.5 = ((bf16[96,4,128]{2,1,0:T(4,128)(2,1)}), bf16[96,4,128]{2,1,0:T(4,128)(2,1)S(1)}, u32[]{:S(2)}, u32[]{:S(2)}) async-start(bf16[96,4,128]{2,1,0:T(4,128)(2,1)} %reshape.153), calls=%async_computation.5 | async-start | bytes 196608 | tf_op jit(solution)/shard_map/all_to_all | solution.py:126

commit v5 on v3

--- a/solution.py
+++ b/solution.py
@@ -97,17 +97,13 @@
 
     payload = jnp.concatenate([tokens, cotangent], axis=1)
     outgoing = jnp.dot(placer, payload, preferred_element_type=jnp.float32).astype(jnp.bfloat16)
-    feat_rows = outgoing.reshape(groups, capacity * 2 * piece // BLOCK, BLOCK)
-    pair_rows = jnp.broadcast_to(
-        slot_pairs.astype(jnp.bfloat16).reshape(groups, capacity, 1), (groups, capacity, BLOCK)
-    )
-    used = feat_rows.shape[1] + capacity
-    tile_rows = -(-used // 16) * 16
-    filler = jnp.zeros((groups, tile_rows - used, BLOCK), jnp.bfloat16)
-    outgoing = jnp.concatenate([feat_rows, pair_rows, filler], axis=1)
-    arrived = lax.all_to_all(outgoing, "dp", split_axis=0, concat_axis=0, tiled=True)
-    feats = arrived[:, :feat_rows.shape[1], :].reshape(slot_count, 2 * piece)
-    pairs_here = arrived[:, feat_rows.shape[1]:used, 0].reshape(slot_count).astype(jnp.int32)
+    pair_cols = jnp.broadcast_to(slot_pairs.astype(jnp.bfloat16)[:, None], (slot_count, BLOCK))
+    outgoing = jnp.concatenate([outgoing, pair_cols], axis=1)
+    arrived = lax.all_to_all(
+        outgoing.reshape(groups, capacity, -1), "dp", split_axis=0, concat_axis=0, tiled=True
+    ).reshape(slot_count, -1)
+    feats = arrived[:, :2 * piece]
+    pairs_here = arrived[:, 2 * piece].astype(jnp.int32)
 
     both = jnp.stack([feats[:, :piece], feats[:, piece:]])
     gathered = lax.all_gather(both, "tensor", axis=0, tiled=False)

time: 182 us -> 176 us (0.967)
  blocking collectives: 78.2 us -> 73.6 us
    all_to_all x1, blocking collectives: 44.8 us -> 40.2 us  [per_device(): lax.all_to_all(outgoing.reshape(groups, capacity, -1), 'dp', split_axis=0...]
where the time goes in v5:
time: 176 us
  blocking collectives  73.6 us (42%)
  waiting for transfers between devices  33.9 us (19%)
  Pallas kernels  27.7 us (16%)
  between operations  14.3 us (8%)
  local copies, waits for them, and re-layouts  9.76 us (6%)
  starting transfers between devices  7.13 us (4%)
  other arithmetic  6.59 us (4%)
  matrix products  2.72 us (2%)
    all_to_all x1, blocking collectives, per_device(): lax.all_to_all(outgoing.reshape(groups, capacity, -1), 'dp', split_axis=0...  40.2 us
    all_to_all x1, blocking collectives, per_device(): lax.all_to_all(back, 'dp', split_axis=0, concat_axis=0, tiled=True)  33.3 us
    pallas_call x4, Pallas kernels, masked_product(): pl.pallas_call(functools.partial(masked_kernel, per=per, turned=turned, p...  27.7 us
    all_to_all x2, waiting for transfers between devices, settle(): lax.all_to_all(part, 'tensor', split_axis=0, concat_axis=0, tiled=True)  17.4 us
    all_gather x1, waiting for transfers between devices, per_device(): gathered = lax.all_gather(both, 'tensor', axis=0, tiled=False)  16.4 us
    all_to_all x2, starting transfers between devices, settle(): lax.all_to_all(part, 'tensor', split_axis=0, concat_axis=0, tiled=True)  7.09 us
    reshape x4, local copies, waits for them, and re-layouts, picked_masks(): looked = looked.reshape(pairs_here.shape[0], blocks_out, BLOCK)  3.81 us
  transfers between devices with their start and end apart: 3, of which 3 were waited for; matrix products, arithmetic and copies ran while one was open for 5% of the time, Pallas kernels for 4%

profile of v5, /device:TPU:8, one launch (start us, length us, event | category | flops | bytes accessed | tf_op | source)
XLA Modules:
  0.0 175.7 jit_solution(6496748452349086299)
XLA Ops:
  7.2 0.7 and_select_fusion
  8.5 1.1 convolution_convert_fusion.4
  9.8 40.2 %all_to_all.20 = bf16[96,2,640]{2,1,0:T(2,128)(2,1)S(1)} all-to-all(bf16[96,2,640]{2,1,0:T(2,128)(2,1)S(1)} %reshape.123), channel_id=1, replica_groups=mesh['dp'=96,'tensor'=8] {'dp'}, dimensions={0} | all-to-all | bytes 491520 | tf_op jit(solution)/shard_map/all_to_all | solution.py:102
  50.1 0.7 pad_maximum_fusion.1
  51.3 0.4 copy.45
  51.9 0.8 fusion.12.e_ref
  52.7 0.9 fusion.4.e_ref
  53.7 0.3 fusion.3
  54.0 0.8 copy.62
  54.8 0.3 fusion.2
  55.2 0.8 copy.63
  56.0 0.4 fusion
  56.4 1.1 copy.61
  57.5 16.4 %all-gather.3.cloned.1.call-done = bf16[16,192,256]{2,1,0:T(8,128)(2,1)} async-done(((bf16[2,192,256]{2,1,0:T(8,128)(2,1)}), bf16[16,192,256]{2,1,0:T(8,128)(2,1)}) %all-gather.3.cloned.1.call-update) | async-done | bytes 1572880 | tf_op jit(solution)/shard_map/all_gather | solution.py:109
  73.9 1.5 fusion.30
  75.4 1.0 copy.53
  76.4 1.0 copy.50
  77.4 7.0 %shard_map.88 = f32[192,1024]{1,0:T(8,128)} custom-call(bf16[192,2048]{1,0:T(8,128)(2,1)} %bitcast.73, bf16[8,192,128]{2,1,0:T(8,128)(2,1)} %bitcast.81, bf16[128,2048]{1,0:T(8,128)(2,1)} %fusion.4.e_ref, bf16[1024,2048]{1,0:T(8,128)(2,1)} %bitcast.69), custom_call_target="tpu_custom_call" | custom-call | tf_op jit(solution)/shard_map/pallas_call | solution.py:66
  84.4 6.8 %shard_map.86 = f32[192,1024]{1,0:T(8,128)} custom-call(bf16[192,2048]{1,0:T(8,128)(2,1)} %bitcast.72, bf16[8,192,128]{2,1,0:T(8,128)(2,1)} %bitcast.82, bf16[128,2048]{1,0:T(8,128)(2,1)} %fusion.4.e_ref, bf16[2048,1024]{1,0:T(8,128)(2,1)} %w_ref.3), custom_call_target="tpu_custom_call" | custom-call | tf_op jit(solution)/shard_map/pallas_call | solution.py:66
  91.2 2.6 %multiply_convert_fusion = (bf16[192,1024]{1,0:T(8,128)(2,1)}, bf16[192,1024]{1,0:T(8,128)(2,1)}) fusion(f32[192,1024]{1,0:T(8,128)} %shard_map.86, f32[192,1024]{1,0:T(8,128)S(1)} %copy-done), kind=kLoop, calls=%fused_computation.23 | loop fusion | flops 4325376 | bytes 2359296 | tf_op jit(solution)/shard_map/convert_element_type | solution.py:122
  93.8 7.0 %shard_map.87 = bf16[8,192,256]{2,1,0:T(8,128)(2,1)} custom-call(bf16[192,1024]{1,0:T(8,128)(2,1)} %get-tuple-element.4.x_ref, bf16[16,192,128]{2,1,0:T(8,128)(2,1)} %bitcast.71, bf16[128,1024]{1,0:T(8,128)(2,1)} %fusion.12.e_ref, bf16[1024,2048]{1,0:T(8,128)(2,1)} %bitcast.70), custom_call_target="tpu_custom_call" | custom-call | tf_op jit(solution)/shard_map/pallas_call | solution.py:66
  100.8 3.5 %all-to-all-start.1 = ((bf16[8,192,256]{2,1,0:T(8,128)(2,1)}), bf16[8,192,256]{2,1,0:T(8,128)(2,1)S(1)}, u32[]{:S(2)}, u32[]{:S(2)}) async-start(bf16[8,192,256]{2,1,0:T(8,128)(2,1)} %shard_map.87), calls=%async_computation.1 | async-start | bytes 1572864 | tf_op jit(solution)/shard_map/all_to_all | solution.py:81
  104.5 0.4 fusion.1
  104.9 1.1 copy.60
  106.0 6.9 %shard_map.89 = bf16[8,192,256]{2,1,0:T(8,128)(2,1)} custom-call(bf16[192,1024]{1,0:T(8,128)(2,1)} %get-tuple-element.5.x_ref, bf16[16,192,128]{2,1,0:T(8,128)(2,1)} %bitcast.74, bf16[128,1024]{1,0:T(8,128)(2,1)} %fusion.12.e_ref, bf16[2048,1024]{1,0:T(8,128)(2,1)} %w_ref.3), custom_call_target="tpu_custom_call" | custom-call | tf_op jit(solution)/shard_map/pallas_call | solution.py:66
  112.9 4.5 %all-to-all-done.1 = bf16[8,192,256]{2,1,0:T(8,128)(2,1)S(1)} async-done(((bf16[8,192,256]{2,1,0:T(8,128)(2,1)}), bf16[8,192,256]{2,1,0:T(8,128)(2,1)S(1)}, u32[]{:S(2)}, u32[]{:S(2)}) %all-to-all-start.1) | async-done | bytes 786464 | tf_op jit(solution)/shard_map/all_to_all | solution.py:81
  117.4 3.5 %all-to-all-start.2 = ((bf16[8,192,256]{2,1,0:T(8,128)(2,1)}), bf16[8,192,256]{2,1,0:T(8,128)(2,1)S(1)}, u32[]{:S(2)}, u32[]{:S(2)}) async-start(bf16[8,192,256]{2,1,0:T(8,128)(2,1)} %shard_map.89), calls=%async_computation.2 | async-start | bytes 1572864 | tf_op jit(solution)/shard_map/all_to_all | solution.py:81
  121.1 12.9 %all-to-all-done.2 = bf16[8,192,256]{2,1,0:T(8,128)(2,1)S(1)} async-done(((bf16[8,192,256]{2,1,0:T(8,128)(2,1)}), bf16[8,192,256]{2,1,0:T(8,128)(2,1)S(1)}, u32[]{:S(2)}, u32[]{:S(2)}) %all-to-all-start.2) | async-done | bytes 786464 | tf_op jit(solution)/shard_map/all_to_all | solution.py:81
  134.2 0.2 copy.43
  134.5 33.3 %all_to_all.21 = bf16[96,8,128]{2,1,0:T(8,128)(2,1)S(1)} all-to-all(bf16[96,8,128]{2,1,0:T(8,128)(2,1)S(1)} %reshape.129), channel_id=1, replica_groups=mesh['dp'=96,'tensor'=8] {'dp'}, dimensions={0} | all-to-all | bytes 393216 | tf_op jit(solution)/shard_map/all_to_all | solution.py:133
  168.0 0.2 convolution_convert_fusion.5
  168.2 0.7 fusion.31
  (40 shorter events, 2.3 us)
Async XLA Ops:
  7.2 66.7 %all-gather.3.cloned.1.call-start = ((), (), s32[]{:S(2)}) async-start(), calls=%async_computation.4 | async-start | bytes 1769472 | tf_op jit(solution)/shard_map/all_gather | solution.py:109
  9.5 41.3 %copy-start.1 = (s32[100,8,16]{0,2,1:T(8,128)S(1)}, s32[100,8,16]{0,2,1:T(8,128)}, u32[]{:S(2)}) copy-start(s32[100,8,16]{0,2,1:T(8,128)} %param.11) | copy-start | bytes 153604
  9.5 41.3 %copy-start.2 = (s32[100,16,8]{0,2,1:T(8,128)S(1)}, s32[100,16,8]{0,2,1:T(8,128)}, u32[]{:S(2)}) copy-start(s32[100,16,8]{0,2,1:T(8,128)} %param.10) | copy-start | bytes 153604
  84.4 6.8 %copy-start = (f32[192,1024]{1,0:T(8,128)S(1)}, f32[192,1024]{1,0:T(8,128)}, u32[]{:S(2)}) copy-start(f32[192,1024]{1,0:T(8,128)} %shard_map.88) | copy-start | bytes 2359300
  100.8 16.6 %all-to-all-start.1 = ((bf16[8,192,256]{2,1,0:T(8,128)(2,1)}), bf16[8,192,256]{2,1,0:T(8,128)(2,1)S(1)}, u32[]{:S(2)}, u32[]{:S(2)}) async-start(bf16[8,192,256]{2,1,0:T(8,128)(2,1)} %shard_map.87), calls=%async_computation.1 | async-start | bytes 1572864 | tf_op jit(solution)/shard_map/all_to_all | solution.py:81
  117.4 16.6 %all-to-all-start.2 = ((bf16[8,192,256]{2,1,0:T(8,128)(2,1)}), bf16[8,192,256]{2,1,0:T(8,128)(2,1)S(1)}, u32[]{:S(2)}, u32[]{:S(2)}) async-start(bf16[8,192,256]{2,1,0:T(8,128)(2,1)} %shard_map.89), calls=%async_computation.2 | async-start | bytes 1572864 | tf_op jit(solution)/shard_map/all_to_all | solution.py:81
Sparse Core Ops, SparseCore 0:
  51.0 22.8 all-gather.2

commit v6 on v5

--- a/solution.py
+++ b/solution.py
@@ -105,10 +105,10 @@
     feats = arrived[:, :2 * piece]
     pairs_here = arrived[:, 2 * piece].astype(jnp.int32)
 
-    both = jnp.stack([feats[:, :piece], feats[:, piece:]])
-    gathered = lax.all_gather(both, "tensor", axis=0, tiled=False)
+    gathered = lax.all_gather(feats, "tensor", axis=0, tiled=False)
     shards = gathered.shape[0]
-    gathered = jnp.transpose(gathered, (1, 2, 0, 3)).reshape(2, slot_count, shards * piece)
+    gathered = gathered.reshape(shards, slot_count, 2, piece)
+    gathered = jnp.transpose(gathered, (2, 1, 0, 3)).reshape(2, slot_count, shards * piece)
     rows_in, grad_rows = gathered[0], gathered[1]
 
     up_fwd, up_in = picked_masks(up_mask, pairs_here, (0, 2, 1))

time: 176 us -> 182 us (1.034)
  local copies, waits for them, and re-layouts: 9.76 us -> 16.1 us
    slice x1 -> x3, local copies, waits for them, and re-layouts: 1.5 us -> 4.56 us  [per_device(): rows_in, grad_rows = (gathered[0], gathered[1])]
    reshape x0 -> x1, local copies, waits for them, and re-layouts: none -> 2.36 us  [per_device(): gathered = gathered.reshape(shards, slot_count, 2, piece)]
where the time goes in v6:
time: 182 us; the launch traced here: 181 us
  blocking collectives  73.7 us (40%)
  waiting for transfers between devices  33.5 us (18%)
  Pallas kernels  27.8 us (15%)
  local copies, waits for them, and re-layouts  16.1 us (9%)
  between operations  14.3 us (8%)
  starting transfers between devices  7.31 us (4%)
  other arithmetic  5.87 us (3%)
  matrix products  2.72 us (1%)
    all_to_all x1, blocking collectives, per_device(): lax.all_to_all(outgoing.reshape(groups, capacity, -1), 'dp', split_axis=0...  40.4 us
    all_to_all x1, blocking collectives, per_device(): lax.all_to_all(back, 'dp', split_axis=0, concat_axis=0, tiled=True)  33.3 us
    pallas_call x4, Pallas kernels, masked_product(): pl.pallas_call(functools.partial(masked_kernel, per=per, turned=turned, p...  27.8 us
    all_gather x1, waiting for transfers between devices, per_device(): gathered = lax.all_gather(feats, 'tensor', axis=0, tiled=False)  17 us
    all_to_all x2, waiting for transfers between devices, settle(): lax.all_to_all(part, 'tensor', split_axis=0, concat_axis=0, tiled=True)  16.6 us
    all_to_all x2, starting transfers between devices, settle(): lax.all_to_all(part, 'tensor', split_axis=0, concat_axis=0, tiled=True)  7.27 us
    slice x3, local copies, waits for them, and re-layouts, per_device(): rows_in, grad_rows = (gathered[0], gathered[1])  4.56 us
    reshape x4, local copies, waits for them, and re-layouts, picked_masks(): looked = looked.reshape(pairs_here.shape[0], blocks_out, BLOCK)  3.81 us
  transfers between devices with their start and end apart: 3, of which 3 were waited for; matrix products, arithmetic and copies ran while one was open for 5% of the time, Pallas kernels for 4%

profile of v6, /device:TPU:8, one launch (start us, length us, event | category | flops | bytes accessed | tf_op | source)
XLA Modules:
  0.0 181.3 jit_solution(7225692286406812276)
XLA Ops:
  7.2 0.7 and_select_fusion
  8.5 1.1 convolution_convert_fusion.4
  9.8 40.4 %all_to_all.20 = bf16[96,2,640]{2,1,0:T(2,128)(2,1)S(1)} all-to-all(bf16[96,2,640]{2,1,0:T(2,128)(2,1)S(1)} %reshape.126), channel_id=1, replica_groups=mesh['dp'=96,'tensor'=8] {'dp'}, dimensions={0} | all-to-all | bytes 491520 | tf_op jit(solution)/shard_map/all_to_all | solution.py:102
  50.3 0.7 slice.26
  51.5 0.8 fusion.12.e_ref
  52.3 0.9 fusion.4.e_ref
  53.3 0.3 fusion.2
  53.6 0.8 copy.54
  54.7 0.8 copy.53
  55.6 0.4 fusion.1
  56.0 1.1 copy.51
  57.1 17.0 %all-gather.3.cloned.1.call-done = bf16[1536,512]{1,0:T(8,128)(2,1)} async-done(((bf16[192,512]{1,0:T(8,128)(2,1)}), bf16[1536,512]{1,0:T(8,128)(2,1)}) %all-gather.3.cloned.1.call-update) | async-done | bytes 1572880 | tf_op jit(solution)/shard_map/all_gather | solution.py:108
  74.0 2.4 %reshape.128 = bf16[8,192,2,256]{3,2,1,0:T(2,128)(2,1)S(1)} reshape(bf16[1536,512]{1,0:T(8,128)(2,1)} %all-gather.3.cloned.1.call-done) | data formatting | bytes 3145728 | tf_op jit(solution)/shard_map/reshape | solution.py:110
  76.4 2.9 %fusion.30 = (bf16[1,192,8,256]{3,0,1,2:T(2,128)(2,1)S(1)}, bf16[1,192,8,256]{3,0,1,2:T(2,128)(2,1)S(1)}) fusion(bf16[2,192,8,256]{3,0,1,2:T(2,128)(2,1)S(1)} %bitcast.63), kind=kLoop, calls=%fused_computation.65 | loop fusion | bytes 3145728 | tf_op jit(solution)/shard_map/slice | solution.py:112
  79.3 0.8 copy.28
  80.1 1.1 copy.43
  81.2 0.8 copy.33
  82.1 1.1 copy.46
  83.2 6.8 %shard_map.86 = f32[192,1024]{1,0:T(8,128)} custom-call(bf16[192,2048]{1,0:T(8,128)(2,1)} %bitcast.65, bf16[8,192,128]{2,1,0:T(8,128)(2,1)} %bitcast.73, bf16[128,2048]{1,0:T(8,128)(2,1)} %fusion.4.e_ref, bf16[2048,1024]{1,0:T(8,128)(2,1)} %w_ref.3), custom_call_target="tpu_custom_call" | custom-call | tf_op jit(solution)/shard_map/pallas_call | solution.py:66
  89.9 7.1 %shard_map.88 = f32[192,1024]{1,0:T(8,128)} custom-call(bf16[192,2048]{1,0:T(8,128)(2,1)} %bitcast.66, bf16[8,192,128]{2,1,0:T(8,128)(2,1)} %bitcast.74, bf16[128,2048]{1,0:T(8,128)(2,1)} %fusion.4.e_ref, bf16[1024,2048]{1,0:T(8,128)(2,1)} %bitcast.61), custom_call_target="tpu_custom_call" | custom-call | tf_op jit(solution)/shard_map/pallas_call | solution.py:66
  97.0 2.6 %multiply_convert_fusion = (bf16[192,1024]{1,0:T(8,128)(2,1)}, bf16[192,1024]{1,0:T(8,128)(2,1)}) fusion(f32[192,1024]{1,0:T(8,128)S(1)} %copy-done, f32[192,1024]{1,0:T(8,128)} %shard_map.88), kind=kLoop, calls=%fused_computation.23 | loop fusion | flops 4325376 | bytes 2359296 | tf_op jit(solution)/shard_map/convert_element_type | solution.py:122
  99.6 6.9 %shard_map.89 = bf16[8,192,256]{2,1,0:T(8,128)(2,1)} custom-call(bf16[192,1024]{1,0:T(8,128)(2,1)} %get-tuple-element.5.x_ref, bf16[16,192,128]{2,1,0:T(8,128)(2,1)} %bitcast.64, bf16[128,1024]{1,0:T(8,128)(2,1)} %fusion.12.e_ref, bf16[2048,1024]{1,0:T(8,128)(2,1)} %w_ref.3), custom_call_target="tpu_custom_call" | custom-call | tf_op jit(solution)/shard_map/pallas_call | solution.py:66
  106.5 3.7 %all-to-all-start.2 = ((bf16[8,192,256]{2,1,0:T(8,128)(2,1)}), bf16[8,192,256]{2,1,0:T(8,128)(2,1)S(1)}, u32[]{:S(2)}, u32[]{:S(2)}) async-start(bf16[8,192,256]{2,1,0:T(8,128)(2,1)} %shard_map.89), calls=%async_computation.2 | async-start | bytes 1572864 | tf_op jit(solution)/shard_map/all_to_all | solution.py:81
  110.2 0.4 copy.38
  110.8 0.4 fusion
  111.3 1.1 copy.52
  112.4 7.1 %shard_map.87 = bf16[8,192,256]{2,1,0:T(8,128)(2,1)} custom-call(bf16[192,1024]{1,0:T(8,128)(2,1)} %get-tuple-element.4.x_ref, bf16[16,192,128]{2,1,0:T(8,128)(2,1)} %bitcast.67, bf16[128,1024]{1,0:T(8,128)(2,1)} %fusion.12.e_ref, bf16[1024,2048]{1,0:T(8,128)(2,1)} %bitcast.62), custom_call_target="tpu_custom_call" | custom-call | tf_op jit(solution)/shard_map/pallas_call | solution.py:66
  119.4 3.7 %all-to-all-done.2 = bf16[8,192,256]{2,1,0:T(8,128)(2,1)S(1)} async-done(((bf16[8,192,256]{2,1,0:T(8,128)(2,1)}), bf16[8,192,256]{2,1,0:T(8,128)(2,1)S(1)}, u32[]{:S(2)}, u32[]{:S(2)}) %all-to-all-start.2) | async-done | bytes 786464 | tf_op jit(solution)/shard_map/all_to_all | solution.py:81
  123.1 3.5 %all-to-all-start.1 = ((bf16[8,192,256]{2,1,0:T(8,128)(2,1)}), bf16[8,192,256]{2,1,0:T(8,128)(2,1)S(1)}, u32[]{:S(2)}, u32[]{:S(2)}) async-start(bf16[8,192,256]{2,1,0:T(8,128)(2,1)} %shard_map.87), calls=%async_computation.1 | async-start | bytes 1572864 | tf_op jit(solution)/shard_map/all_to_all | solution.py:81
  126.7 12.9 %all-to-all-done.1 = bf16[8,192,256]{2,1,0:T(8,128)(2,1)S(1)} async-done(((bf16[8,192,256]{2,1,0:T(8,128)(2,1)}), bf16[8,192,256]{2,1,0:T(8,128)(2,1)S(1)}, u32[]{:S(2)}, u32[]{:S(2)}) %all-to-all-start.1) | async-done | bytes 786464 | tf_op jit(solution)/shard_map/all_to_all | solution.py:81
  140.2 33.3 %all_to_all.21 = bf16[96,8,128]{2,1,0:T(8,128)(2,1)S(1)} all-to-all(bf16[96,8,128]{2,1,0:T(8,128)(2,1)S(1)} %reshape.133), channel_id=1, replica_groups=mesh['dp'=96,'tensor'=8] {'dp'}, dimensions={0} | all-to-all | bytes 393216 | tf_op jit(solution)/shard_map/all_to_all | solution.py:133
  173.8 0.7 fusion.31
  (42 shorter events, 3.0 us)
Async XLA Ops:
  7.2 66.8 %all-gather.3.cloned.1.call-start = ((), (), s32[]{:S(2)}) async-start(), calls=%async_computation.4 | async-start | bytes 1769472 | tf_op jit(solution)/shard_map/all_gather | solution.py:108
  8.0 43.0 %copy-start.1 = (s32[100,16,8]{0,2,1:T(8,128)S(1)}, s32[100,16,8]{0,2,1:T(8,128)}, u32[]{:S(2)}) copy-start(s32[100,16,8]{0,2,1:T(8,128)} %param.10) | copy-start | bytes 153604
  9.8 41.5 %copy-start.2 = (s32[100,8,16]{0,2,1:T(8,128)S(1)}, s32[100,8,16]{0,2,1:T(8,128)}, u32[]{:S(2)}) copy-start(s32[100,8,16]{0,2,1:T(8,128)} %param.11) | copy-start | bytes 153604
  89.9 7.1 %copy-start = (f32[192,1024]{1,0:T(8,128)S(1)}, f32[192,1024]{1,0:T(8,128)}, u32[]{:S(2)}) copy-start(f32[192,1024]{1,0:T(8,128)} %shard_map.86) | copy-start | bytes 2359300
  106.5 16.6 %all-to-all-start.2 = ((bf16[8,192,256]{2,1,0:T(8,128)(2,1)}), bf16[8,192,256]{2,1,0:T(8,128)(2,1)S(1)}, u32[]{:S(2)}, u32[]{:S(2)}) async-start(bf16[8,192,256]{2,1,0:T(8,128)(2,1)} %shard_map.89), calls=%async_computation.2 | async-start | bytes 1572864 | tf_op jit(solution)/shard_map/all_to_all | solution.py:81
  123.1 16.6 %all-to-all-start.1 = ((bf16[8,192,256]{2,1,0:T(8,128)(2,1)}), bf16[8,192,256]{2,1,0:T(8,128)(2,1)S(1)}, u32[]{:S(2)}, u32[]{:S(2)}) async-start(bf16[8,192,256]{2,1,0:T(8,128)(2,1)} %shard_map.87), calls=%async_computation.1 | async-start | bytes 1572864 | tf_op jit(solution)/shard_map/all_to_all | solution.py:81
Sparse Core Ops, SparseCore 0:
  51.1 22.8 all-gather.2

commit v7 on v5

--- a/solution.py
+++ b/solution.py
@@ -23,24 +23,26 @@
     return jnp.transpose(looked, (1, 0, 2)), blocks_in
 
 
-def masked_kernel(x_ref, m_ref, e_ref, w_ref, o_ref, *, per, turned, piece):
-    x = x_ref[...]
+def masked_kernel(x_ref, m_ref, w_ref, o_ref, *, per, turned, piece, blocks_in):
+    accs = [None] * per
+    for i in range(blocks_in):
+        xi = x_ref[:, i * BLOCK:(i + 1) * BLOCK]
+        if not turned:
+            y = jnp.dot(xi, w_ref[i * BLOCK:(i + 1) * BLOCK, :], preferred_element_type=jnp.float32)
+        for b in range(per):
+            if turned:
+                w = w_ref[b * BLOCK:(b + 1) * BLOCK, i * BLOCK:(i + 1) * BLOCK]
+                yb = lax.dot_general(xi, w, (((1,), (1,)), ((), ())), preferred_element_type=jnp.float32)
+            else:
+                yb = y[:, b * BLOCK:(b + 1) * BLOCK]
+            term = yb * m_ref[b, :, i:i + 1]
+            accs[b] = term if accs[b] is None else accs[b] + term
     for b in range(per):
-        spread = jnp.dot(m_ref[b], e_ref[...], preferred_element_type=jnp.float32).astype(x.dtype)
-        masked = x * spread
-        if turned:
-            w = w_ref[b * BLOCK:(b + 1) * BLOCK, :]
-            acc = lax.dot_general(
-                masked, w, (((1,), (1,)), ((), ())), preferred_element_type=jnp.float32
-            )
-        else:
-            w = w_ref[:, b * BLOCK:(b + 1) * BLOCK]
-            acc = jnp.dot(masked, w, preferred_element_type=jnp.float32)
         if piece:
             at = b * BLOCK
-            o_ref[at // piece, :, at % piece:at % piece + BLOCK] = acc.astype(o_ref.dtype)
+            o_ref[at // piece, :, at % piece:at % piece + BLOCK] = accs[b].astype(o_ref.dtype)
         else:
-            o_ref[:, b * BLOCK:(b + 1) * BLOCK] = acc.astype(o_ref.dtype)
+            o_ref[:, b * BLOCK:(b + 1) * BLOCK] = accs[b].astype(o_ref.dtype)
 
 
 def masked_product(x, masks, blocks_in, weight, turned, out_dtype, piece=0):
@@ -49,10 +51,7 @@
     per = max(1, blocks_out // STEPS)
     steps = blocks_out // per
     cols = per * BLOCK
-    blk = width // blocks_in
-    expand = (
-        jnp.arange(width, dtype=jnp.int32)[None, :] // blk == jnp.arange(BLOCK, dtype=jnp.int32)[:, None]
-    ).astype(x.dtype)
+    masks = masks.astype(jnp.float32)
     if turned:
         w_spec = pl.BlockSpec((cols, width), lambda j: (j, 0))
     else:
@@ -64,17 +63,16 @@
         out_spec = pl.BlockSpec((rows, cols), lambda j: (0, j))
         out_shape = (rows, blocks_out * BLOCK)
     return pl.pallas_call(
-        functools.partial(masked_kernel, per=per, turned=turned, piece=piece),
+        functools.partial(masked_kernel, per=per, turned=turned, piece=piece, blocks_in=blocks_in),
         grid=(steps,),
         in_specs=[
             pl.BlockSpec((rows, width), lambda j: (0, 0)),
             pl.BlockSpec((per, rows, BLOCK), lambda j: (j, 0, 0)),
-            pl.BlockSpec((BLOCK, width), lambda j: (0, 0)),
             w_spec,
         ],
         out_specs=out_spec,
         out_shape=jax.ShapeDtypeStruct(out_shape, out_dtype),
-    )(x, masks, expand, weight)
+    )(x, masks, weight)
 
 
 def settle(part):

time: 176 us -> 176 us (level)
    convert_element_type x0 -> x4, local copies, waits for them, and re-layouts: none -> 4.49 us  [masked_product(): masks = masks.astype(jnp.float32)]
    reshape x4 -> x0, local copies, waits for them, and re-layouts: 3.81 us -> none  [picked_masks(): looked = looked.reshape(pairs_here.shape[0], blocks_out, BLOCK)]
  transfers between devices with their start and end apart: 3 -> 3, of which waited for: 3 -> 3; matrix products, arithmetic and copies ran while one was open for 5% -> 4% of each run, Pallas kernels for 4% -> 4%
where the time goes in v7:
time: 176 us; the launch traced here: 175 us
  blocking collectives  73.6 us (42%)
  waiting for transfers between devices  35 us (20%)
  Pallas kernels  26.7 us (15%)
  between operations  14.3 us (8%)
  local copies, waits for them, and re-layouts  10.4 us (6%)
  starting transfers between devices  7.13 us (4%)
  other arithmetic  4.89 us (3%)
  matrix products  2.72 us (2%)
    all_to_all x1, blocking collectives, per_device(): lax.all_to_all(outgoing.reshape(groups, capacity, -1), 'dp', split_axis=0...  40.2 us
    all_to_all x1, blocking collectives, per_device(): lax.all_to_all(back, 'dp', split_axis=0, concat_axis=0, tiled=True)  33.3 us
    pallas_call x4, Pallas kernels, masked_product(): pl.pallas_call(functools.partial(masked_kernel, per=per, turned=turned, p...  26.7 us
    all_gather x1, waiting for transfers between devices, per_device(): gathered = lax.all_gather(both, 'tensor', axis=0, tiled=False)  17.7 us
    all_to_all x2, waiting for transfers between devices, settle(): lax.all_to_all(part, 'tensor', split_axis=0, concat_axis=0, tiled=True)  17.4 us
    all_to_all x2, starting transfers between devices, settle(): lax.all_to_all(part, 'tensor', split_axis=0, concat_axis=0, tiled=True)  7.09 us
    convert_element_type x4, local copies, waits for them, and re-layouts, masked_product(): masks = masks.astype(jnp.float32)  4.49 us
  transfers between devices with their start and end apart: 3, of which 3 were waited for; matrix products, arithmetic and copies ran while one was open for 4% of the time, Pallas kernels for 4%

profile of v7, /device:TPU:8, one launch (start us, length us, event | category | flops | bytes accessed | tf_op | source)
XLA Modules:
  0.0 174.8 jit_solution(13001723173536158945)
XLA Ops:
  7.2 0.7 and_select_fusion
  8.0 0.2 reduce_window_sum.11
  8.5 1.1 convolution_convert_fusion.4
  9.8 40.2 %all_to_all.20 = bf16[96,2,640]{2,1,0:T(2,128)(2,1)S(1)} all-to-all(bf16[96,2,640]{2,1,0:T(2,128)(2,1)S(1)} %reshape.49), channel_id=1, replica_groups=mesh['dp'=96,'tensor'=8] {'dp'}, dimensions={0} | all-to-all | bytes 491520 | tf_op jit(solution)/shard_map/all_to_all | solution.py:100
  50.1 0.7 pad_maximum_fusion.1
  50.9 0.2 copy.44
  51.3 0.4 copy.45
  52.0 0.3 fusion.5
  52.4 0.9 copy.62
  53.3 0.3 fusion.7
  53.6 0.9 copy.63
  54.5 0.4 fusion.2
  54.9 1.3 copy.61
  56.3 17.7 %all-gather.3.cloned.1.call-done = bf16[16,192,256]{2,1,0:T(8,128)(2,1)} async-done(((bf16[2,192,256]{2,1,0:T(8,128)(2,1)}), bf16[16,192,256]{2,1,0:T(8,128)(2,1)}) %all-gather.3.cloned.1.call-update) | async-done | bytes 1572880 | tf_op jit(solution)/shard_map/all_gather | solution.py:107
  73.9 1.5 fusion.26
  75.4 1.0 copy.53
  76.4 1.0 copy.50
  77.4 6.8 %shard_map.88 = f32[192,1024]{1,0:T(8,128)} custom-call(bf16[192,2048]{1,0:T(8,128)(2,1)} %bitcast.75, f32[8,192,128]{2,1,0:T(8,128)} %bitcast.73, bf16[1024,2048]{1,0:T(8,128)(2,1)} %bitcast.69), custom_call_target="tpu_custom_call" | custom-call | tf_op jit(solution)/shard_map/pallas_call | solution.py:65
  84.2 6.6 %shard_map.86 = f32[192,1024]{1,0:T(8,128)} custom-call(bf16[192,2048]{1,0:T(8,128)(2,1)} %bitcast.76, f32[8,192,128]{2,1,0:T(8,128)} %bitcast.74, bf16[2048,1024]{1,0:T(8,128)(2,1)} %w_ref.3), custom_call_target="tpu_custom_call" | custom-call | tf_op jit(solution)/shard_map/pallas_call | solution.py:65
  90.8 2.6 %multiply_convert_fusion = (bf16[192,1024]{1,0:T(8,128)(2,1)}, bf16[192,1024]{1,0:T(8,128)(2,1)}) fusion(f32[192,1024]{1,0:T(8,128)} %shard_map.86, f32[192,1024]{1,0:T(8,128)S(1)} %copy-done), kind=kLoop, calls=%fused_computation.27 | loop fusion | flops 4325376 | bytes 2359296 | tf_op jit(solution)/shard_map/convert_element_type | solution.py:120
  93.3 6.5 %shard_map.87 = bf16[8,192,256]{2,1,0:T(8,128)(2,1)} custom-call(bf16[192,1024]{1,0:T(8,128)(2,1)} %get-tuple-element.4.x_ref, f32[16,192,128]{2,1,0:T(8,128)} %bitcast.71, bf16[1024,2048]{1,0:T(8,128)(2,1)} %bitcast.70), custom_call_target="tpu_custom_call" | custom-call | tf_op jit(solution)/shard_map/pallas_call | solution.py:65
  99.9 3.5 %all-to-all-start.1 = ((bf16[8,192,256]{2,1,0:T(8,128)(2,1)}), bf16[8,192,256]{2,1,0:T(8,128)(2,1)S(1)}, u32[]{:S(2)}, u32[]{:S(2)}) async-start(bf16[8,192,256]{2,1,0:T(8,128)(2,1)} %shard_map.87), calls=%async_computation.1 | async-start | bytes 1572864 | tf_op jit(solution)/shard_map/all_to_all | solution.py:79
  103.6 0.4 fusion.3
  104.0 1.3 copy.60
  105.3 6.7 %shard_map.89 = bf16[8,192,256]{2,1,0:T(8,128)(2,1)} custom-call(bf16[192,1024]{1,0:T(8,128)(2,1)} %get-tuple-element.5.x_ref, f32[16,192,128]{2,1,0:T(8,128)} %bitcast.72, bf16[2048,1024]{1,0:T(8,128)(2,1)} %w_ref.3), custom_call_target="tpu_custom_call" | custom-call | tf_op jit(solution)/shard_map/pallas_call | solution.py:65
  112.0 4.4 %all-to-all-done.1 = bf16[8,192,256]{2,1,0:T(8,128)(2,1)S(1)} async-done(((bf16[8,192,256]{2,1,0:T(8,128)(2,1)}), bf16[8,192,256]{2,1,0:T(8,128)(2,1)S(1)}, u32[]{:S(2)}, u32[]{:S(2)}) %all-to-all-start.1) | async-done | bytes 786464 | tf_op jit(solution)/shard_map/all_to_all | solution.py:79
  116.5 3.5 %all-to-all-start.2 = ((bf16[8,192,256]{2,1,0:T(8,128)(2,1)}), bf16[8,192,256]{2,1,0:T(8,128)(2,1)S(1)}, u32[]{:S(2)}, u32[]{:S(2)}) async-start(bf16[8,192,256]{2,1,0:T(8,128)(2,1)} %shard_map.89), calls=%async_computation.2 | async-start | bytes 1572864 | tf_op jit(solution)/shard_map/all_to_all | solution.py:79
  120.2 12.9 %all-to-all-done.2 = bf16[8,192,256]{2,1,0:T(8,128)(2,1)S(1)} async-done(((bf16[8,192,256]{2,1,0:T(8,128)(2,1)}), bf16[8,192,256]{2,1,0:T(8,128)(2,1)S(1)}, u32[]{:S(2)}, u32[]{:S(2)}) %all-to-all-start.2) | async-done | bytes 786464 | tf_op jit(solution)/shard_map/all_to_all | solution.py:79
  133.2 0.2 copy.43
  133.6 33.3 %all_to_all.21 = bf16[96,8,128]{2,1,0:T(8,128)(2,1)S(1)} all-to-all(bf16[96,8,128]{2,1,0:T(8,128)(2,1)S(1)} %reshape.51), channel_id=1, replica_groups=mesh['dp'=96,'tensor'=8] {'dp'}, dimensions={0} | all-to-all | bytes 393216 | tf_op jit(solution)/shard_map/all_to_all | solution.py:131
  167.0 0.2 convolution_convert_fusion.5
  167.3 0.7 fusion.27
  (36 shorter events, 1.9 us)
Async XLA Ops:
  7.2 66.8 %all-gather.3.cloned.1.call-start = ((), (), s32[]{:S(2)}) async-start(), calls=%async_computation.4 | async-start | bytes 1769472 | tf_op jit(solution)/shard_map/all_gather | solution.py:107
  9.5 41.3 %copy-start.1 = (s32[100,8,16]{0,2,1:T(8,128)S(1)}, s32[100,8,16]{0,2,1:T(8,128)}, u32[]{:S(2)}) copy-start(s32[100,8,16]{0,2,1:T(8,128)} %param.11) | copy-start | bytes 153604
  9.5 41.3 %copy-start.2 = (s32[100,16,8]{0,2,1:T(8,128)S(1)}, s32[100,16,8]{0,2,1:T(8,128)}, u32[]{:S(2)}) copy-start(s32[100,16,8]{0,2,1:T(8,128)} %param.10) | copy-start | bytes 153604
  84.2 6.6 %copy-start = (f32[192,1024]{1,0:T(8,128)S(1)}, f32[192,1024]{1,0:T(8,128)}, u32[]{:S(2)}) copy-start(f32[192,1024]{1,0:T(8,128)} %shard_map.88) | copy-start | bytes 2359300
  99.9 16.6 %all-to-all-start.1 = ((bf16[8,192,256]{2,1,0:T(8,128)(2,1)}), bf16[8,192,256]{2,1,0:T(8,128)(2,1)S(1)}, u32[]{:S(2)}, u32[]{:S(2)}) async-start(bf16[8,192,256]{2,1,0:T(8,128)(2,1)} %shard_map.87), calls=%async_computation.1 | async-start | bytes 1572864 | tf_op jit(solution)/shard_map/all_to_all | solution.py:79
  116.5 16.6 %all-to-all-start.2 = ((bf16[8,192,256]{2,1,0:T(8,128)(2,1)}), bf16[8,192,256]{2,1,0:T(8,128)(2,1)S(1)}, u32[]{:S(2)}, u32[]{:S(2)}) async-start(bf16[8,192,256]{2,1,0:T(8,128)(2,1)} %shard_map.89), calls=%async_computation.2 | async-start | bytes 1572864 | tf_op jit(solution)/shard_map/all_to_all | solution.py:79
Sparse Core Ops, SparseCore 0:
  51.0 22.8 all-gather.2

commit v8 on v7

--- a/solution.py
+++ b/solution.py
@@ -23,7 +23,7 @@
     return jnp.transpose(looked, (1, 0, 2)), blocks_in
 
 
-def masked_kernel(x_ref, m_ref, w_ref, o_ref, *, per, turned, piece, blocks_in):
+def masked_kernel(x_ref, m_ref, w_ref, o_ref, *act_ref, per, turned, piece, blocks_in):
     accs = [None] * per
     for i in range(blocks_in):
         xi = x_ref[:, i * BLOCK:(i + 1) * BLOCK]
@@ -43,9 +43,11 @@
             o_ref[at // piece, :, at % piece:at % piece + BLOCK] = accs[b].astype(o_ref.dtype)
         else:
             o_ref[:, b * BLOCK:(b + 1) * BLOCK] = accs[b].astype(o_ref.dtype)
+        if act_ref:
+            act_ref[0][:, b * BLOCK:(b + 1) * BLOCK] = jax.nn.gelu(accs[b]).astype(act_ref[0].dtype)
 
 
-def masked_product(x, masks, blocks_in, weight, turned, out_dtype, piece=0):
+def masked_product(x, masks, blocks_in, weight, turned, out_dtype, piece=0, act=False):
     rows, width = x.shape
     blocks_out = masks.shape[0]
     per = max(1, blocks_out // STEPS)
@@ -70,8 +72,12 @@
             pl.BlockSpec((per, rows, BLOCK), lambda j: (j, 0, 0)),
             w_spec,
         ],
-        out_specs=out_spec,
-        out_shape=jax.ShapeDtypeStruct(out_shape, out_dtype),
+        out_specs=[out_spec, out_spec] if act else out_spec,
+        out_shape=(
+            [jax.ShapeDtypeStruct(out_shape, out_dtype), jax.ShapeDtypeStruct(out_shape, x.dtype)]
+            if act
+            else jax.ShapeDtypeStruct(out_shape, out_dtype)
+        ),
     )(x, masks, weight)
 
 
@@ -115,9 +121,8 @@
     down_bwd, down_out = picked_masks(down_mask, pairs_here, (0, 1, 2))
     down_local = down_weight[0]
 
-    before_act = masked_product(rows_in, up_fwd, up_in, up_weight, False, jnp.float32)
-    activated, backward_function = jax.vjp(jax.nn.gelu, before_act)
-    hidden = activated.astype(jnp.bfloat16)
+    before_act, hidden = masked_product(rows_in, up_fwd, up_in, up_weight, False, jnp.float32, act=True)
+    _, backward_function = jax.vjp(jax.nn.gelu, before_act)
     mixed_part = masked_product(hidden, down_fwd, down_in, down_local, False, jnp.bfloat16, piece)
     mixed_sum = settle(mixed_part)
     grad_hidden = masked_product(grad_rows, down_bwd, down_out, down_local, True, jnp.float32)

time: 176 us -> 176 us (level)
  no operation moved by 1% of the time
where the time goes in v8:
time: 176 us; the launch traced here: 175 us
  blocking collectives  73.6 us (42%)
  waiting for transfers between devices  35.2 us (20%)
  Pallas kernels  26.8 us (15%)
  between operations  14.3 us (8%)
  local copies, waits for them, and re-layouts  10.4 us (6%)
  starting transfers between devices  7.13 us (4%)
  other arithmetic  4.74 us (3%)
  matrix products  2.72 us (2%)
    all_to_all x1, blocking collectives, per_device(): lax.all_to_all(outgoing.reshape(groups, capacity, -1), 'dp', split_axis=0...  40.2 us
    all_to_all x1, blocking collectives, per_device(): lax.all_to_all(back, 'dp', split_axis=0, concat_axis=0, tiled=True)  33.3 us
    pallas_call x4, Pallas kernels, masked_product(): pl.pallas_call(functools.partial(masked_kernel, per=per, turned=turned, p...  26.8 us
    all_gather x1, waiting for transfers between devices, per_device(): gathered = lax.all_gather(both, 'tensor', axis=0, tiled=False)  18.2 us
    all_to_all x2, waiting for transfers between devices, settle(): lax.all_to_all(part, 'tensor', split_axis=0, concat_axis=0, tiled=True)  17 us
    all_to_all x2, starting transfers between devices, settle(): lax.all_to_all(part, 'tensor', split_axis=0, concat_axis=0, tiled=True)  7.09 us
    convert_element_type x4, local copies, waits for them, and re-layouts, masked_product(): masks = masks.astype(jnp.float32)  4.49 us
  transfers between devices with their start and end apart: 3, of which 3 were waited for; matrix products, arithmetic and copies ran while one was open for 4% of the time, Pallas kernels for 4%

profile of v8, /device:TPU:8, one launch (start us, length us, event | category | flops | bytes accessed | tf_op | source)
XLA Modules:
  0.0 175.0 jit_solution(3702967533590228717)
XLA Ops:
  7.2 0.7 and_select_fusion
  8.0 0.2 reduce_window_sum.11
  8.5 1.1 convolution_convert_fusion.4
  9.8 40.2 %all_to_all.20 = bf16[96,2,640]{2,1,0:T(2,128)(2,1)S(1)} all-to-all(bf16[96,2,640]{2,1,0:T(2,128)(2,1)S(1)} %reshape.49), channel_id=1, replica_groups=mesh['dp'=96,'tensor'=8] {'dp'}, dimensions={0} | all-to-all | bytes 491520 | tf_op jit(solution)/shard_map/all_to_all | solution.py:106
  50.1 0.7 pad_maximum_fusion.1
  50.9 0.2 copy.44
  51.5 0.3 fusion.5
  51.8 0.9 copy.62
  52.8 0.3 fusion.7
  53.1 0.9 copy.63
  54.0 0.4 fusion.3
  54.4 1.3 copy.60
  55.7 18.2 %all-gather.3.cloned.1.call-done = bf16[16,192,256]{2,1,0:T(8,128)(2,1)} async-done(((bf16[2,192,256]{2,1,0:T(8,128)(2,1)}), bf16[16,192,256]{2,1,0:T(8,128)(2,1)}) %all-gather.3.cloned.1.call-update) | async-done | bytes 1572880 | tf_op jit(solution)/shard_map/all_gather | solution.py:113
  73.9 1.5 fusion.26
  75.4 1.0 copy.53
  76.4 1.0 copy.50
  77.4 6.7 %shard_map.88 = f32[192,1024]{1,0:T(8,128)} custom-call(bf16[192,2048]{1,0:T(8,128)(2,1)} %bitcast.74, f32[8,192,128]{2,1,0:T(8,128)} %bitcast.73, bf16[1024,2048]{1,0:T(8,128)(2,1)} %bitcast.69), custom_call_target="tpu_custom_call" | custom-call | tf_op jit(solution)/shard_map/pallas_call | solution.py:67
  84.1 6.8 %shard_map.86 = (f32[192,1024]{1,0:T(8,128)}, bf16[192,1024]{1,0:T(8,128)(2,1)}) custom-call(bf16[192,2048]{1,0:T(8,128)(2,1)} %bitcast.78, f32[8,192,128]{2,1,0:T(8,128)} %bitcast.77, bf16[2048,1024]{1,0:T(8,128)(2,1)} %w_ref.3), custom_call_target="tpu_custom_call" | custom-call | tf_op jit(solution)/shard_map/pallas_call | solution.py:67
  90.9 2.4 %fusion.14.x_ref = bf16[192,1024]{1,0:T(8,128)(2,1)} fusion(f32[192,1024]{1,0:T(8,128)} %get-tuple-element.5, f32[192,1024]{1,0:T(8,128)S(1)} %copy-done), kind=kLoop, calls=%fused_computation.24 | loop fusion | flops 3932160 | bytes 1966080 | tf_op jit(solution)/shard_map/convert_element_type | solution.py:129
  93.3 6.7 %shard_map.89 = bf16[8,192,256]{2,1,0:T(8,128)(2,1)} custom-call(bf16[192,1024]{1,0:T(8,128)(2,1)} %fusion.14.x_ref, f32[16,192,128]{2,1,0:T(8,128)} %bitcast.71, bf16[2048,1024]{1,0:T(8,128)(2,1)} %w_ref.3), custom_call_target="tpu_custom_call" | custom-call | tf_op jit(solution)/shard_map/pallas_call | solution.py:67
  100.1 3.5 %all-to-all-start.2 = ((bf16[8,192,256]{2,1,0:T(8,128)(2,1)}), bf16[8,192,256]{2,1,0:T(8,128)(2,1)S(1)}, u32[]{:S(2)}, u32[]{:S(2)}) async-start(bf16[8,192,256]{2,1,0:T(8,128)(2,1)} %shard_map.89), calls=%async_computation.2 | async-start | bytes 1572864 | tf_op jit(solution)/shard_map/all_to_all | solution.py:85
  103.6 0.4 copy.45
  104.3 0.4 fusion.2
  104.7 1.3 copy.61
  106.0 6.6 %shard_map.87 = bf16[8,192,256]{2,1,0:T(8,128)(2,1)} custom-call(bf16[192,1024]{1,0:T(8,128)(2,1)} %get-tuple-element.4.x_ref, f32[16,192,128]{2,1,0:T(8,128)} %bitcast.72, bf16[1024,2048]{1,0:T(8,128)(2,1)} %bitcast.70), custom_call_target="tpu_custom_call" | custom-call | tf_op jit(solution)/shard_map/pallas_call | solution.py:67
  112.6 4.1 %all-to-all-done.2 = bf16[8,192,256]{2,1,0:T(8,128)(2,1)S(1)} async-done(((bf16[8,192,256]{2,1,0:T(8,128)(2,1)}), bf16[8,192,256]{2,1,0:T(8,128)(2,1)S(1)}, u32[]{:S(2)}, u32[]{:S(2)}) %all-to-all-start.2) | async-done | bytes 786464 | tf_op jit(solution)/shard_map/all_to_all | solution.py:85
  116.7 3.5 %all-to-all-start.1 = ((bf16[8,192,256]{2,1,0:T(8,128)(2,1)}), bf16[8,192,256]{2,1,0:T(8,128)(2,1)S(1)}, u32[]{:S(2)}, u32[]{:S(2)}) async-start(bf16[8,192,256]{2,1,0:T(8,128)(2,1)} %shard_map.87), calls=%async_computation.1 | async-start | bytes 1572864 | tf_op jit(solution)/shard_map/all_to_all | solution.py:85
  120.3 12.9 %all-to-all-done.1 = bf16[8,192,256]{2,1,0:T(8,128)(2,1)S(1)} async-done(((bf16[8,192,256]{2,1,0:T(8,128)(2,1)}), bf16[8,192,256]{2,1,0:T(8,128)(2,1)S(1)}, u32[]{:S(2)}, u32[]{:S(2)}) %all-to-all-start.1) | async-done | bytes 786464 | tf_op jit(solution)/shard_map/all_to_all | solution.py:85
  133.4 0.2 copy.43
  133.8 33.3 %all_to_all.21 = bf16[96,8,128]{2,1,0:T(8,128)(2,1)S(1)} all-to-all(bf16[96,8,128]{2,1,0:T(8,128)(2,1)S(1)} %reshape.51), channel_id=1, replica_groups=mesh['dp'=96,'tensor'=8] {'dp'}, dimensions={0} | all-to-all | bytes 393216 | tf_op jit(solution)/shard_map/all_to_all | solution.py:136
  167.2 0.2 convolution_convert_fusion.5
  167.5 0.7 fusion.27
  (36 shorter events, 1.9 us)
Async XLA Ops:
  7.2 66.8 %all-gather.3.cloned.1.call-start = ((), (), s32[]{:S(2)}) async-start(), calls=%async_computation.4 | async-start | bytes 1769472 | tf_op jit(solution)/shard_map/all_gather | solution.py:113
  9.5 41.3 %copy-start.2 = (s32[100,8,16]{0,2,1:T(8,128)S(1)}, s32[100,8,16]{0,2,1:T(8,128)}, u32[]{:S(2)}) copy-start(s32[100,8,16]{0,2,1:T(8,128)} %param.11) | copy-start | bytes 153604
  9.5 41.3 %copy-start.1 = (s32[100,16,8]{0,2,1:T(8,128)S(1)}, s32[100,16,8]{0,2,1:T(8,128)}, u32[]{:S(2)}) copy-start(s32[100,16,8]{0,2,1:T(8,128)} %param.10) | copy-start | bytes 153604
  84.1 6.8 %copy-start = (f32[192,1024]{1,0:T(8,128)S(1)}, f32[192,1024]{1,0:T(8,128)}, u32[]{:S(2)}) copy-start(f32[192,1024]{1,0:T(8,128)} %shard_map.88) | copy-start | bytes 2359300
  100.1 16.6 %all-to-all-start.2 = ((bf16[8,192,256]{2,1,0:T(8,128)(2,1)}), bf16[8,192,256]{2,1,0:T(8,128)(2,1)S(1)}, u32[]{:S(2)}, u32[]{:S(2)}) async-start(bf16[8,192,256]{2,1,0:T(8,128)(2,1)} %shard_map.89), calls=%async_computation.2 | async-start | bytes 1572864 | tf_op jit(solution)/shard_map/all_to_all | solution.py:85
  116.7 16.6 %all-to-all-start.1 = ((bf16[8,192,256]{2,1,0:T(8,128)(2,1)}), bf16[8,192,256]{2,1,0:T(8,128)(2,1)S(1)}, u32[]{:S(2)}, u32[]{:S(2)}) async-start(bf16[8,192,256]{2,1,0:T(8,128)(2,1)} %shard_map.87), calls=%async_computation.1 | async-start | bytes 1572864 | tf_op jit(solution)/shard_map/all_to_all | solution.py:85
Sparse Core Ops, SparseCore 0:
  51.0 22.8 all-gather.2

commit v9 on v8

--- a/solution.py
+++ b/solution.py
@@ -23,7 +23,10 @@
     return jnp.transpose(looked, (1, 0, 2)), blocks_in
 
 
-def masked_kernel(x_ref, m_ref, w_ref, o_ref, *act_ref, per, turned, piece, blocks_in):
+def masked_kernel(x_ref, m_ref, w_ref, *refs, per, turned, piece, blocks_in, act, grad):
+    pre_ref = refs[0] if grad else None
+    o_ref = refs[1] if grad else refs[0]
+    act_ref = refs[-1:] if act else ()
     accs = [None] * per
     for i in range(blocks_in):
         xi = x_ref[:, i * BLOCK:(i + 1) * BLOCK]
@@ -41,13 +44,16 @@
         if piece:
             at = b * BLOCK
             o_ref[at // piece, :, at % piece:at % piece + BLOCK] = accs[b].astype(o_ref.dtype)
+        elif grad:
+            _, backward_function = jax.vjp(jax.nn.gelu, pre_ref[:, b * BLOCK:(b + 1) * BLOCK])
+            o_ref[:, b * BLOCK:(b + 1) * BLOCK] = backward_function(accs[b])[0].astype(o_ref.dtype)
         else:
             o_ref[:, b * BLOCK:(b + 1) * BLOCK] = accs[b].astype(o_ref.dtype)
         if act_ref:
             act_ref[0][:, b * BLOCK:(b + 1) * BLOCK] = jax.nn.gelu(accs[b]).astype(act_ref[0].dtype)
 
 
-def masked_product(x, masks, blocks_in, weight, turned, out_dtype, piece=0, act=False):
+def masked_product(x, masks, blocks_in, weight, turned, out_dtype, piece=0, act=False, grad_of=None):
     rows, width = x.shape
     blocks_out = masks.shape[0]
     per = max(1, blocks_out // STEPS)
@@ -64,21 +70,25 @@
     else:
         out_spec = pl.BlockSpec((rows, cols), lambda j: (0, j))
         out_shape = (rows, blocks_out * BLOCK)
+    grad = grad_of is not None
+    extra = [grad_of] if grad else []
     return pl.pallas_call(
-        functools.partial(masked_kernel, per=per, turned=turned, piece=piece, blocks_in=blocks_in),
+        functools.partial(
+            masked_kernel, per=per, turned=turned, piece=piece, blocks_in=blocks_in, act=act, grad=grad
+        ),
         grid=(steps,),
         in_specs=[
             pl.BlockSpec((rows, width), lambda j: (0, 0)),
             pl.BlockSpec((per, rows, BLOCK), lambda j: (j, 0, 0)),
             w_spec,
-        ],
+        ] + [out_spec] * len(extra),
         out_specs=[out_spec, out_spec] if act else out_spec,
         out_shape=(
             [jax.ShapeDtypeStruct(out_shape, out_dtype), jax.ShapeDtypeStruct(out_shape, x.dtype)]
             if act
             else jax.ShapeDtypeStruct(out_shape, out_dtype)
         ),
-    )(x, masks, weight)
+    )(x, masks, weight, *extra)
 
 
 def settle(part):
@@ -122,11 +132,11 @@
     down_local = down_weight[0]
 
     before_act, hidden = masked_product(rows_in, up_fwd, up_in, up_weight, False, jnp.float32, act=True)
-    _, backward_function = jax.vjp(jax.nn.gelu, before_act)
     mixed_part = masked_product(hidden, down_fwd, down_in, down_local, False, jnp.bfloat16, piece)
     mixed_sum = settle(mixed_part)
-    grad_hidden = masked_product(grad_rows, down_bwd, down_out, down_local, True, jnp.float32)
-    grad_pre = backward_function(grad_hidden)[0].astype(jnp.bfloat16)
+    grad_pre = masked_product(
+        grad_rows, down_bwd, down_out, down_local, True, jnp.bfloat16, grad_of=before_act
+    )
     input_part = masked_product(grad_pre, up_bwd, up_out, up_weight, True, jnp.bfloat16, piece)
     input_sum = settle(input_part)
 

time: 176 us -> 174 us (0.989)
  other arithmetic: 4.74 us -> 2.34 us
    convert_element_type x1 -> x0, other arithmetic: 2.4 us -> none  [per_device(): grad_pre = backward_function(grad_hidden)[0].astype(jnp.bfloat16)]
where the time goes in v9:
time: 174 us; the launch traced here: 173 us
  blocking collectives  73.6 us (42%)
  waiting for transfers between devices  35.2 us (20%)
  Pallas kernels  27 us (16%)
  between operations  14.3 us (8%)
  local copies, waits for them, and re-layouts  10.4 us (6%)
  starting transfers between devices  7.13 us (4%)
  matrix products  2.72 us (2%)
  other arithmetic  2.34 us (1%)
    all_to_all x1, blocking collectives, per_device(): lax.all_to_all(outgoing.reshape(groups, capacity, -1), 'dp', split_axis=0...  40.2 us
    all_to_all x1, blocking collectives, per_device(): lax.all_to_all(back, 'dp', split_axis=0, concat_axis=0, tiled=True)  33.3 us
    pallas_call x4, Pallas kernels, masked_product(): pl.pallas_call(functools.partial(masked_kernel, per=per, turned=turned, p...  27 us
    all_gather x1, waiting for transfers between devices, per_device(): gathered = lax.all_gather(both, 'tensor', axis=0, tiled=False)  18.2 us
    all_to_all x2, waiting for transfers between devices, settle(): lax.all_to_all(part, 'tensor', split_axis=0, concat_axis=0, tiled=True)  17 us
    all_to_all x2, starting transfers between devices, settle(): lax.all_to_all(part, 'tensor', split_axis=0, concat_axis=0, tiled=True)  7.09 us
    convert_element_type x4, local copies, waits for them, and re-layouts, masked_product(): masks = masks.astype(jnp.float32)  4.49 us
  transfers between devices with their start and end apart: 3, of which 3 were waited for; matrix products, arithmetic and copies ran while one was open for 4% of the time, Pallas kernels for 4%

profile of v9, /device:TPU:8, one launch (start us, length us, event | category | flops | bytes accessed | tf_op | source)
XLA Modules:
  0.0 172.8 jit_solution(14574560503986544513)
XLA Ops:
  7.2 0.7 and_select_fusion
  8.0 0.2 reduce_window_sum.11
  8.1 0.2 select_reduce_fusion.1
  8.5 1.1 convolution_convert_fusion.4
  9.8 40.2 %all_to_all.20 = bf16[96,2,640]{2,1,0:T(2,128)(2,1)S(1)} all-to-all(bf16[96,2,640]{2,1,0:T(2,128)(2,1)S(1)} %reshape.49), channel_id=1, replica_groups=mesh['dp'=96,'tensor'=8] {'dp'}, dimensions={0} | all-to-all | bytes 491520 | tf_op jit(solution)/shard_map/all_to_all | solution.py:116
  50.1 0.7 pad_maximum_fusion.1
  50.9 0.2 copy.44
  51.5 0.3 fusion.5
  51.8 0.9 copy.62
  52.8 0.3 fusion.7
  53.1 0.9 copy.63
  54.0 0.4 fusion.3
  54.4 1.3 copy.60
  55.7 18.2 %all-gather.3.cloned.1.call-done = bf16[16,192,256]{2,1,0:T(8,128)(2,1)} async-done(((bf16[2,192,256]{2,1,0:T(8,128)(2,1)}), bf16[16,192,256]{2,1,0:T(8,128)(2,1)}) %all-gather.3.cloned.1.call-update) | async-done | bytes 1572880 | tf_op jit(solution)/shard_map/all_gather | solution.py:123
  73.9 1.5 fusion.19
  75.4 1.0 copy.53
  76.4 1.0 copy.50
  77.4 6.7 %shard_map.86 = (f32[192,1024]{1,0:T(8,128)}, bf16[192,1024]{1,0:T(8,128)(2,1)}) custom-call(bf16[192,2048]{1,0:T(8,128)(2,1)} %bitcast.78, f32[8,192,128]{2,1,0:T(8,128)} %bitcast.76, bf16[2048,1024]{1,0:T(8,128)(2,1)} %w_ref.3), custom_call_target="tpu_custom_call" | custom-call | tf_op jit(solution)/shard_map/pallas_call | solution.py:75
  84.1 7.1 %shard_map.88.x_ref = bf16[192,1024]{1,0:T(8,128)(2,1)} custom-call(bf16[192,2048]{1,0:T(8,128)(2,1)} %bitcast.77, f32[8,192,128]{2,1,0:T(8,128)} %bitcast.75, bf16[1024,2048]{1,0:T(8,128)(2,1)} %bitcast.69, f32[192,1024]{1,0:T(8,128)} %get-tuple-element.5.refs_0_), custom_call_target="tpu_custom_call" | custom-call | tf_op jit(solution)/shard_map/pallas_call | solution.py:75
  91.1 6.8 %shard_map.89 = bf16[8,192,256]{2,1,0:T(8,128)(2,1)} custom-call(bf16[192,1024]{1,0:T(8,128)(2,1)} %shard_map.88.x_ref, f32[16,192,128]{2,1,0:T(8,128)} %bitcast.71, bf16[2048,1024]{1,0:T(8,128)(2,1)} %w_ref.3), custom_call_target="tpu_custom_call" | custom-call | tf_op jit(solution)/shard_map/pallas_call | solution.py:75
  97.9 3.5 %all-to-all-start.2 = ((bf16[8,192,256]{2,1,0:T(8,128)(2,1)}), bf16[8,192,256]{2,1,0:T(8,128)(2,1)S(1)}, u32[]{:S(2)}, u32[]{:S(2)}) async-start(bf16[8,192,256]{2,1,0:T(8,128)(2,1)} %shard_map.89), calls=%async_computation.2 | async-start | bytes 1572864 | tf_op jit(solution)/shard_map/all_to_all | solution.py:95
  101.5 0.4 copy.45
  102.1 0.4 fusion.2
  102.5 1.3 copy.61
  103.8 6.6 %shard_map.87 = bf16[8,192,256]{2,1,0:T(8,128)(2,1)} custom-call(bf16[192,1024]{1,0:T(8,128)(2,1)} %get-tuple-element.4.x_ref, f32[16,192,128]{2,1,0:T(8,128)} %bitcast.72, bf16[1024,2048]{1,0:T(8,128)(2,1)} %bitcast.70), custom_call_target="tpu_custom_call" | custom-call | tf_op jit(solution)/shard_map/pallas_call | solution.py:75
  110.4 4.1 %all-to-all-done.2 = bf16[8,192,256]{2,1,0:T(8,128)(2,1)S(1)} async-done(((bf16[8,192,256]{2,1,0:T(8,128)(2,1)}), bf16[8,192,256]{2,1,0:T(8,128)(2,1)S(1)}, u32[]{:S(2)}, u32[]{:S(2)}) %all-to-all-start.2) | async-done | bytes 786464 | tf_op jit(solution)/shard_map/all_to_all | solution.py:95
  114.5 3.5 %all-to-all-start.1 = ((bf16[8,192,256]{2,1,0:T(8,128)(2,1)}), bf16[8,192,256]{2,1,0:T(8,128)(2,1)S(1)}, u32[]{:S(2)}, u32[]{:S(2)}) async-start(bf16[8,192,256]{2,1,0:T(8,128)(2,1)} %shard_map.87), calls=%async_computation.1 | async-start | bytes 1572864 | tf_op jit(solution)/shard_map/all_to_all | solution.py:95
  118.2 12.9 %all-to-all-done.1 = bf16[8,192,256]{2,1,0:T(8,128)(2,1)S(1)} async-done(((bf16[8,192,256]{2,1,0:T(8,128)(2,1)}), bf16[8,192,256]{2,1,0:T(8,128)(2,1)S(1)}, u32[]{:S(2)}, u32[]{:S(2)}) %all-to-all-start.1) | async-done | bytes 786464 | tf_op jit(solution)/shard_map/all_to_all | solution.py:95
  131.2 0.2 copy.43
  131.6 33.3 %all_to_all.21 = bf16[96,8,128]{2,1,0:T(8,128)(2,1)S(1)} all-to-all(bf16[96,8,128]{2,1,0:T(8,128)(2,1)S(1)} %reshape.51), channel_id=1, replica_groups=mesh['dp'=96,'tensor'=8] {'dp'}, dimensions={0} | all-to-all | bytes 393216 | tf_op jit(solution)/shard_map/all_to_all | solution.py:146
  165.0 0.2 convolution_convert_fusion.5
  165.3 0.7 fusion.20
  (33 shorter events, 1.7 us)
Async XLA Ops:
  7.2 66.8 %all-gather.3.cloned.1.call-start = ((), (), s32[]{:S(2)}) async-start(), calls=%async_computation.4 | async-start | bytes 1769472 | tf_op jit(solution)/shard_map/all_gather | solution.py:123
  9.5 41.3 %copy-start.1 = (s32[100,8,16]{0,2,1:T(8,128)S(1)}, s32[100,8,16]{0,2,1:T(8,128)}, u32[]{:S(2)}) copy-start(s32[100,8,16]{0,2,1:T(8,128)} %param.11) | copy-start | bytes 153604
  9.5 41.3 %copy-start = (s32[100,16,8]{0,2,1:T(8,128)S(1)}, s32[100,16,8]{0,2,1:T(8,128)}, u32[]{:S(2)}) copy-start(s32[100,16,8]{0,2,1:T(8,128)} %param.10) | copy-start | bytes 153604
  97.9 16.6 %all-to-all-start.2 = ((bf16[8,192,256]{2,1,0:T(8,128)(2,1)}), bf16[8,192,256]{2,1,0:T(8,128)(2,1)S(1)}, u32[]{:S(2)}, u32[]{:S(2)}) async-start(bf16[8,192,256]{2,1,0:T(8,128)(2,1)} %shard_map.89), calls=%async_computation.2 | async-start | bytes 1572864 | tf_op jit(solution)/shard_map/all_to_all | solution.py:95
  114.5 16.6 %all-to-all-start.1 = ((bf16[8,192,256]{2,1,0:T(8,128)(2,1)}), bf16[8,192,256]{2,1,0:T(8,128)(2,1)S(1)}, u32[]{:S(2)}, u32[]{:S(2)}) async-start(bf16[8,192,256]{2,1,0:T(8,128)(2,1)} %shard_map.87), calls=%async_computation.1 | async-start | bytes 1572864 | tf_op jit(solution)/shard_map/all_to_all | solution.py:95
Sparse Core Ops, SparseCore 0:
  51.0 22.8 all-gather.2

commit v10 on v9

--- a/solution.py
+++ b/solution.py
@@ -7,7 +7,7 @@
 from jax.sharding import PartitionSpec as P
 
 BLOCK = 128
-STEPS = 4
+STEPS = 2
 
 
 def picked_masks(mask_table, pairs_here, order):

time: 174 us -> 173 us (level)
  no operation moved by 1% of the time
where the time goes in v10:
time: 173 us
  blocking collectives  73.6 us (43%)
  waiting for transfers between devices  35.5 us (21%)
  Pallas kernels  26.4 us (15%)
  between operations  14.3 us (8%)
  local copies, waits for them, and re-layouts  10.4 us (6%)
  starting transfers between devices  7.31 us (4%)
  matrix products  2.72 us (2%)
  other arithmetic  2.34 us (1%)
    all_to_all x1, blocking collectives, per_device(): lax.all_to_all(outgoing.reshape(groups, capacity, -1), 'dp', split_axis=0...  40.2 us
    all_to_all x1, blocking collectives, per_device(): lax.all_to_all(back, 'dp', split_axis=0, concat_axis=0, tiled=True)  33.3 us
    pallas_call x4, Pallas kernels, masked_product(): pl.pallas_call(functools.partial(masked_kernel, per=per, turned=turned, p...  26.4 us
    all_gather x1, waiting for transfers between devices, per_device(): gathered = lax.all_gather(both, 'tensor', axis=0, tiled=False)  18.2 us
    all_to_all x2, waiting for transfers between devices, settle(): lax.all_to_all(part, 'tensor', split_axis=0, concat_axis=0, tiled=True)  17.3 us
    all_to_all x2, starting transfers between devices, settle(): lax.all_to_all(part, 'tensor', split_axis=0, concat_axis=0, tiled=True)  7.27 us
    convert_element_type x4, local copies, waits for them, and re-layouts, masked_product(): masks = masks.astype(jnp.float32)  4.49 us
  transfers between devices with their start and end apart: 3, of which 3 were waited for; matrix products, arithmetic and copies ran while one was open for 4% of the time, Pallas kernels for 4%

profile of v10, /device:TPU:8, one launch (start us, length us, event | category | flops | bytes accessed | tf_op | source)
XLA Modules:
  0.0 172.6 jit_solution(18281940642552141068)
XLA Ops:
  7.2 0.7 and_select_fusion
  8.0 0.2 reduce_window_sum.11
  8.1 0.2 select_reduce_fusion.1
  8.5 1.1 convolution_convert_fusion.4
  9.8 40.2 %all_to_all.20 = bf16[96,2,640]{2,1,0:T(2,128)(2,1)S(1)} all-to-all(bf16[96,2,640]{2,1,0:T(2,128)(2,1)S(1)} %reshape.49), channel_id=1, replica_groups=mesh['dp'=96,'tensor'=8] {'dp'}, dimensions={0} | all-to-all | bytes 491520 | tf_op jit(solution)/shard_map/all_to_all | solution.py:116
  50.2 0.7 pad_maximum_fusion.1
  50.9 0.2 copy.44
  51.5 0.3 fusion.5
  51.9 0.9 copy.62
  52.8 0.3 fusion.7
  53.1 0.9 copy.63
  54.0 0.4 fusion.3
  54.4 1.3 copy.60
  55.7 18.2 %all-gather.3.cloned.1.call-done = bf16[16,192,256]{2,1,0:T(8,128)(2,1)} async-done(((bf16[2,192,256]{2,1,0:T(8,128)(2,1)}), bf16[16,192,256]{2,1,0:T(8,128)(2,1)}) %all-gather.3.cloned.1.call-update) | async-done | bytes 1572880 | tf_op jit(solution)/shard_map/all_gather | solution.py:123
  73.9 1.5 fusion.19
  75.4 1.0 copy.53
  76.4 1.0 copy.50
  77.4 6.5 %shard_map.86 = (f32[192,1024]{1,0:T(8,128)}, bf16[192,1024]{1,0:T(8,128)(2,1)}) custom-call(bf16[192,2048]{1,0:T(8,128)(2,1)} %bitcast.78, f32[8,192,128]{2,1,0:T(8,128)} %bitcast.76, bf16[2048,1024]{1,0:T(8,128)(2,1)} %w_ref.3), custom_call_target="tpu_custom_call" | custom-call | tf_op jit(solution)/shard_map/pallas_call | solution.py:75
  83.9 7.3 %shard_map.88.x_ref = bf16[192,1024]{1,0:T(8,128)(2,1)} custom-call(bf16[192,2048]{1,0:T(8,128)(2,1)} %bitcast.77, f32[8,192,128]{2,1,0:T(8,128)} %bitcast.75, bf16[1024,2048]{1,0:T(8,128)(2,1)} %bitcast.69, f32[192,1024]{1,0:T(8,128)} %get-tuple-element.5.refs_0_), custom_call_target="tpu_custom_call" | custom-call | tf_op jit(solution)/shard_map/pallas_call | solution.py:75
  91.2 6.5 %shard_map.89 = bf16[8,192,256]{2,1,0:T(8,128)(2,1)} custom-call(bf16[192,1024]{1,0:T(8,128)(2,1)} %shard_map.88.x_ref, f32[16,192,128]{2,1,0:T(8,128)} %bitcast.71, bf16[2048,1024]{1,0:T(8,128)(2,1)} %w_ref.3), custom_call_target="tpu_custom_call" | custom-call | tf_op jit(solution)/shard_map/pallas_call | solution.py:75
  97.7 3.7 %all-to-all-start.2 = ((bf16[8,192,256]{2,1,0:T(8,128)(2,1)}), bf16[8,192,256]{2,1,0:T(8,128)(2,1)S(1)}, u32[]{:S(2)}, u32[]{:S(2)}) async-start(bf16[8,192,256]{2,1,0:T(8,128)(2,1)} %shard_map.89), calls=%async_computation.2 | async-start | bytes 1572864 | tf_op jit(solution)/shard_map/all_to_all | solution.py:95
  101.4 0.4 copy.45
  102.1 0.4 fusion.2
  102.5 1.3 copy.61
  103.8 6.1 %shard_map.87 = bf16[8,192,256]{2,1,0:T(8,128)(2,1)} custom-call(bf16[192,1024]{1,0:T(8,128)(2,1)} %get-tuple-element.4.x_ref, f32[16,192,128]{2,1,0:T(8,128)} %bitcast.72, bf16[1024,2048]{1,0:T(8,128)(2,1)} %bitcast.70), custom_call_target="tpu_custom_call" | custom-call | tf_op jit(solution)/shard_map/pallas_call | solution.py:75
  109.9 4.4 %all-to-all-done.2 = bf16[8,192,256]{2,1,0:T(8,128)(2,1)S(1)} async-done(((bf16[8,192,256]{2,1,0:T(8,128)(2,1)}), bf16[8,192,256]{2,1,0:T(8,128)(2,1)S(1)}, u32[]{:S(2)}, u32[]{:S(2)}) %all-to-all-start.2) | async-done | bytes 786464 | tf_op jit(solution)/shard_map/all_to_all | solution.py:95
  114.3 3.5 %all-to-all-start.1 = ((bf16[8,192,256]{2,1,0:T(8,128)(2,1)}), bf16[8,192,256]{2,1,0:T(8,128)(2,1)S(1)}, u32[]{:S(2)}, u32[]{:S(2)}) async-start(bf16[8,192,256]{2,1,0:T(8,128)(2,1)} %shard_map.87), calls=%async_computation.1 | async-start | bytes 1572864 | tf_op jit(solution)/shard_map/all_to_all | solution.py:95
  118.0 12.9 %all-to-all-done.1 = bf16[8,192,256]{2,1,0:T(8,128)(2,1)S(1)} async-done(((bf16[8,192,256]{2,1,0:T(8,128)(2,1)}), bf16[8,192,256]{2,1,0:T(8,128)(2,1)S(1)}, u32[]{:S(2)}, u32[]{:S(2)}) %all-to-all-start.1) | async-done | bytes 786464 | tf_op jit(solution)/shard_map/all_to_all | solution.py:95
  131.0 0.2 copy.43
  131.4 33.3 %all_to_all.21 = bf16[96,8,128]{2,1,0:T(8,128)(2,1)S(1)} all-to-all(bf16[96,8,128]{2,1,0:T(8,128)(2,1)S(1)} %reshape.51), channel_id=1, replica_groups=mesh['dp'=96,'tensor'=8] {'dp'}, dimensions={0} | all-to-all | bytes 393216 | tf_op jit(solution)/shard_map/all_to_all | solution.py:146
  164.8 0.2 convolution_convert_fusion.5
  165.1 0.7 fusion.20
  (33 shorter events, 1.7 us)
Async XLA Ops:
  7.2 66.8 %all-gather.3.cloned.1.call-start = ((), (), s32[]{:S(2)}) async-start(), calls=%async_computation.4 | async-start | bytes 1769472 | tf_op jit(solution)/shard_map/all_gather | solution.py:123
  9.5 41.3 %copy-start.1 = (s32[100,8,16]{0,2,1:T(8,128)S(1)}, s32[100,8,16]{0,2,1:T(8,128)}, u32[]{:S(2)}) copy-start(s32[100,8,16]{0,2,1:T(8,128)} %param.11) | copy-start | bytes 153604
  9.5 41.3 %copy-start = (s32[100,16,8]{0,2,1:T(8,128)S(1)}, s32[100,16,8]{0,2,1:T(8,128)}, u32[]{:S(2)}) copy-start(s32[100,16,8]{0,2,1:T(8,128)} %param.10) | copy-start | bytes 153604
  97.7 16.6 %all-to-all-start.2 = ((bf16[8,192,256]{2,1,0:T(8,128)(2,1)}), bf16[8,192,256]{2,1,0:T(8,128)(2,1)S(1)}, u32[]{:S(2)}, u32[]{:S(2)}) async-start(bf16[8,192,256]{2,1,0:T(8,128)(2,1)} %shard_map.89), calls=%async_computation.2 | async-start | bytes 1572864 | tf_op jit(solution)/shard_map/all_to_all | solution.py:95
  114.3 16.6 %all-to-all-start.1 = ((bf16[8,192,256]{2,1,0:T(8,128)(2,1)}), bf16[8,192,256]{2,1,0:T(8,128)(2,1)S(1)}, u32[]{:S(2)}, u32[]{:S(2)}) async-start(bf16[8,192,256]{2,1,0:T(8,128)(2,1)} %shard_map.87), calls=%async_computation.1 | async-start | bytes 1572864 | tf_op jit(solution)/shard_map/all_to_all | solution.py:95
Sparse Core Ops, SparseCore 0:
  51.0 22.8 all-gather.2
